TPU v7x, 32 devices: a whole 2x2x4 slice. The times are simulated.
32 devices in a mesh: row: 4 (over y, x), col: 4 (over z), layer: 2 (over core).
Axes of the slice: x: 2, y: 2, z: 4, core: 2. Of those that a mesh axis runs over, the one named last changes fastest.
Arguments:
- x_blocks: bfloat16 [64, 64, 4, 256], P('col', None, 'row'), may hold values from -1 to 1
- x_cols: int32 [64, 4, 4], P('col', 'row'), may hold values from 0 to 15, as said below
- x_count: int32 [64, 4], P('col', 'row'), may hold values from 1 to 4, as said below
- out_cols: int32 [64, 4, 8], P('col', 'row'), may hold values from 0 to 15, as said below
Outputs:
- product: float32 [64, 64, 4, 512], P('col', None, 'row', 'layer')
Inputs may be any that keep to these rules, and one draw needn't show every extreme that they name: `x_cols`: within one block row and tile the 4 column entries are distinct. For every tile column t, at least one block row R has x_count[R,t] = 4. `out_cols`: within one block row and tile the 8 column entries are distinct.
All inputs are finite; a program needn't handle non-finite values.
Results may differ from a plain program's by a relative error of at most 0.0003.
Values may be sent and summed in bfloat16 or wider, within the bound.
No kernel may reach another device: no remote copies, remote signals or barrier semaphores. Data moves between devices by JAX's collectives and lax.ppermute only.
A program may use at most 64 MiB of HBM per device.

v0:
```python
import functools

import jax
import jax.numpy as jnp
from jax import lax
from jax.experimental import pallas as pl
from jax.experimental.pallas import tpu as pltpu
from jax.sharding import PartitionSpec as P


def step_kernel(a_cols, b_cols, want, a_ref, b_ref, *refs):
    if len(refs) == 7:
        mine_in, theirs_in, mine_ref, theirs_ref, place_ref, sel_ref, slot_of = refs
    else:
        mine_in = theirs_in = None
        mine_ref, theirs_ref, place_ref, sel_ref, slot_of = refs
    width = a_ref.shape[1]
    seg = a_ref.shape[2]
    slots = seg // width
    rows = place_ref.shape[0]
    outs = want.shape[0] // rows
    lane = lax.broadcasted_iota(jnp.int32, (width, 2 * width), 1)
    zero = jnp.zeros((width, 2 * width), b_ref.dtype)

    def fill(k, carry):
        for q in range(slots):
            grp = b_ref[k, :, (q // 2) * 2 * width:(q // 2 + 1) * 2 * width]
            swap = pltpu.roll(grp, width, 1)
            for i in range(2):
                src = grp if i == q % 2 else swap
                keep = lane < width if i == 0 else lane >= width
                place_ref[k, q, i] = jnp.where(keep, src, zero)
        for i in range(2):
            place_ref[k, slots, i] = zero
        return carry

    lax.fori_loop(0, rows, fill, 0)
    for n in range(rows * rows):
        slot_of[n] = jnp.int32(slots)
    for n in range(rows * slots):
        slot_of[(n // slots) * rows + b_cols[n]] = jnp.int32(n % slots)

    def one_row(r, carry):
        for p in range(slots):
            k = a_cols[r * slots + p]
            for g in range(outs // 2):
                picks = []
                for i in range(2):
                    hit = slot_of[k * rows + want[r * outs + 2 * g + i]]
                    picks.append(place_ref[k, hit, i])
                sel_ref[p * width:(p + 1) * width, g * 2 * width:(g + 1) * 2 * width] = picks[0] + picks[1]
        prod = jnp.dot(a_ref[r], sel_ref[...], preferred_element_type=jnp.float32)
        half = prod.shape[1] // 2
        if mine_in is None:
            mine_ref[r] = prod[:, :half]
            theirs_ref[r] = prod[:, half:]
        else:
            mine_ref[r] = mine_in[r] + prod[:, :half]
            theirs_ref[r] = theirs_in[r] + prod[:, half:]
        return carry

    lax.fori_loop(0, rows, one_row, 0)


def one_step(mine, theirs, left, right, a_cols, b_cols, want):
    rows, width, seg = left.shape[0] - 1, left.shape[1], left.shape[2]
    outs = want.shape[0] // rows
    share = outs // 2 * width
    sums = [] if mine is None else [mine, theirs]
    smem = pl.BlockSpec(memory_space=pltpu.SMEM)
    vmem = pl.BlockSpec(memory_space=pltpu.VMEM)
    cost = pl.CostEstimate(
        flops=2 * rows * width * seg * outs * width,
        transcendentals=0,
        bytes_accessed=2 * (left.size + right.size) + 4 * (2 + len(sums)) * rows * width * share,
    )
    return pl.pallas_call(
        step_kernel,
        in_specs=[smem] * 3 + [vmem] * (2 + len(sums)),
        out_specs=[vmem, vmem],
        scratch_shapes=[
            pltpu.VMEM((rows, seg // width + 1, 2, width, 2 * width), right.dtype),
            pltpu.VMEM((seg, outs * width), right.dtype),
            pltpu.SMEM((rows * rows,), jnp.int32),
        ],
        out_shape=[jax.ShapeDtypeStruct((rows, width, share), jnp.float32)] * 2,
        input_output_aliases={5: 0, 6: 1} if sums else {},
        cost_estimate=cost,
    )(a_cols, b_cols, want, left, right, *sums)


def per_device(x_blocks, x_cols, x_count, out_cols):
    row_count, width, _, lanes = x_blocks.shape
    slots = lanes // width
    values = x_blocks[:, :, 0, :]
    slot_of_lane = lax.broadcasted_iota(jnp.int32, (1, 1, lanes), 2) // width
    values = jnp.where(slot_of_lane < x_count[:, :, None], values, jnp.zeros((), values.dtype))
    columns = x_cols[:, 0, :].reshape(-1)
    extra = jnp.zeros((1, width, lanes), values.dtype)
    extra = extra.at[0, 0, :columns.shape[0]].set(columns.astype(values.dtype))
    payload = jnp.concatenate([values, extra], axis=0)

    rows_n = lax.axis_size("row")
    cols_n = lax.axis_size("col")
    layers = lax.axis_size("layer")
    steps = rows_n // layers
    me_r = lax.axis_index("row")
    me_c = lax.axis_index("col")
    me_l = lax.axis_index("layer")

    def flat(r, c, l):
        return (r * cols_n + c) * layers + l

    outs = out_cols.shape[2]
    share = outs // layers
    both = jnp.concatenate([out_cols[:, 0, :], out_cols[:, 0, :]], axis=1)
    want = lax.dynamic_slice_in_dim(both, me_l * share, outs, axis=1).reshape(-1)
    mine = theirs = None
    for s in range(steps):
        left_pairs = []
        right_pairs = []
        for r in range(rows_n):
            for c in range(cols_n):
                for l in range(layers):
                    t = (r + c + s + l * steps) % rows_n
                    left_pairs.append((flat(t, c, l), flat(r, c, l)))
                    right_pairs.append((flat(r, t, l), flat(r, c, l)))
        left = lax.ppermute(payload, ("row", "col", "layer"), left_pairs)
        right = lax.ppermute(payload, ("row", "col", "layer"), right_pairs)
        after = 0 if mine is None else (mine[0, 0, 0] * 0).astype(jnp.int32)
        a_cols = left[row_count, 0, :columns.shape[0]].astype(jnp.int32) + after
        b_cols = right[row_count, 0, :columns.shape[0]].astype(jnp.int32) + after
        mine, theirs = one_step(mine, theirs, left, right, a_cols, b_cols, want)

    got = lax.ppermute(theirs, "layer", [(0, 1), (1, 0)])
    return mine[:, :, None, :] + got[:, :, None, :]


def solution(mesh):
    placed = (
        P("col", None, "row", None),
        P("col", "row", None),
        P("col", "row"),
        P("col", "row", None),
    )
    return jax.shard_map(
        per_device,
        mesh=mesh,
        in_specs=placed,
        out_specs=P("col", None, "row", "layer"),
        check_vma=False,
    )
```

profile of v0, /device:TPU:5, one launch (start us, length us, event | category | flops | bytes accessed | tf_op | source)
XLA Modules:
  0.0 60.1 jit_solution(12486439364179644542)
XLA Ops:
  0.0 0.7 %convert_element_type.35 = bf16[16,1,4]{0,2,1:T(4,128)(2,1)S(1)} convert(s32[16,1,4]{0,2,1:T(4,128)} %param.7) | non-fusion elementwise | flops 64 | bytes 384 | tf_op jit(solution)/shard_map/convert_element_type | solution.py:100
  0.7 0.1 copy.10
  0.8 0.1 convert_element_type.36
  0.9 0.7 %broadcast_compare_fusion = pred[16,256]{1,0:T(8,128)(4,1)S(1)} fusion(s32[256]{0:T(256)S(1)} %and_select_fusion, s32[16]{0:T(128)} %bitcast.24), kind=kLoop, calls=%fused_computation.7 | loop fusion | flops 4096 | bytes 5184 | tf_op jit(solution)/shard_map/lt | solution.py:97
  1.6 0.0 copy-start.4
  1.6 1.1 %bitcast_select_fusion = bf16[16,64,256]{2,1,0:T(8,128)(2,1)S(1)} fusion(bf16[16,64,1,256]{3,1,2,0:T(8,128)(2,1)} %param.6, pred[16,256]{1,0:T(8,128)(4,1)S(1)} %broadcast_compare_fusion), kind=kLoop, calls=%fused_computation.4 | loop fusion | flops 262144 | bytes 1052672 | tf_op jit(solution)/shard_map/jit(_where)/select_n | solution.py:97
  2.8 0.7 %collective-permute-start.2 = (bf16[17,64,256]{2,1,0:T(8,128)(2,1)S(1)}, bf16[17,64,256]{2,1,0:T(8,128)(2,1)S(1)}, u32[]{:S(2)}, u32[]{:S(2)}) collective-permute-start(bf16[17,64,256]{2,1,0:T(8,128)(2,1)S(1)} %fusion.1), channel_id=1, source_target_pairs={{0,0},{5,1},{2,2},{7,3},{4,4},{1,5},{6,6},{3,7},{10,8},{15,9},{12,... | collective-permute-start | bytes 1671176 | tf_op jit(solution)/shard_map/ppermute | solution.py:129
  3.5 5.7 %collective-permute-start.1 = (bf16[17,64,256]{2,1,0:T(8,128)(2,1)S(1)}, bf16[17,64,256]{2,1,0:T(8,128)(2,1)S(1)}, u32[]{:S(2)}, u32[]{:S(2)}) collective-permute-start(bf16[17,64,256]{2,1,0:T(8,128)(2,1)S(1)} %fusion.1), channel_id=1, source_target_pairs={{0,0},{17,1},{10,2},{27,3},{20,4},{5,5},{30,6},{15,7},{8,8},{25,9}... | collective-permute-start | bytes 1671176 | tf_op jit(solution)/shard_map/ppermute | solution.py:128
  9.1 3.9 %collective-permute-start.3 = (bf16[17,64,256]{2,1,0:T(8,128)(2,1)S(1)}, bf16[17,64,256]{2,1,0:T(8,128)(2,1)S(1)}, u32[]{:S(2)}, u32[]{:S(2)}) collective-permute-start(bf16[17,64,256]{2,1,0:T(8,128)(2,1)S(1)} %fusion.1), channel_id=1, source_target_pairs={{2,0},{7,1},{4,2},{1,3},{6,4},{3,5},{0,6},{5,7},{12,8},{9,9},{14,1... | collective-permute-start | bytes 1671176 | tf_op jit(solution)/shard_map/ppermute | solution.py:129
  13.0 2.0 %collective-permute-start = (bf16[17,64,256]{2,1,0:T(8,128)(2,1)S(1)}, bf16[17,64,256]{2,1,0:T(8,128)(2,1)S(1)}, u32[]{:S(2)}, u32[]{:S(2)}) collective-permute-start(bf16[17,64,256]{2,1,0:T(8,128)(2,1)S(1)} %fusion.1), channel_id=1, source_target_pairs={{8,0},{25,1},{18,2},{3,3},{28,4},{13,5},{6,6},{23,7},{16,8},{1,9},... | collective-permute-start | bytes 1671176 | tf_op jit(solution)/shard_map/ppermute | solution.py:128
  15.0 0.0 copy-done.4
  15.0 0.1 copy.11
  15.1 0.6 reshape.125.want
  15.7 0.0 collective-permute-done.2.b_ref
  15.7 0.0 copy-start.2
  15.7 0.6 %fusion.5.b_cols = s32[64]{0:T(128)} fusion(bf16[17,64,256]{2,1,0:T(8,128)(2,1)S(1)} %collective-permute-done.2.b_ref), kind=kLoop, calls=%fused_computation.17 | loop fusion | flops 64 | bytes 384 | tf_op jit(solution)/shard_map/convert_element_type | solution.py:132
  16.3 0.0 collective-permute-done.1.a_ref
  16.3 0.0 copy-start.3
  16.3 0.6 fusion.6.a_cols
  16.9 0.0 copy-done.2
  16.9 0.3 copy-done.3
  17.2 8.1 %shard_map.46 = (f32[16,64,256]{2,1,0:T(8,128)}, f32[16,64,256]{2,1,0:T(8,128)}) custom-call(s32[64]{0:T(128)} %fusion.6.a_cols, s32[64]{0:T(128)} %fusion.5.b_cols, s32[128]{0:T(128)} %reshape.125.want, bf16[17,64,256]{2,1,0:T(8,128)(2,1)} %copy-done.3, bf16[17,64,256]{2,1,0:T(8,128)(2,1)} %copy-done.2), custom_call_target="tpu_custom_call" | custom-call | flops 268435456 | bytes 3211264 | tf_op jit(solution)/shard_map/pallas_call | solution.py:77
  25.3 1.2 %slice.39 = f32[1,1,1]{2,1,0:T(1,128)} slice(f32[16,64,256]{2,1,0:T(8,128)} %get-tuple-element.21.refs_0_), slice={[0:1], [0:1], [0:1]} | slice | bytes 8 | tf_op jit(solution)/shard_map/slice | solution.py:130
  27.1 1.9 %collective-permute-done.3.b_ref = bf16[17,64,256]{2,1,0:T(8,128)(2,1)S(1)} collective-permute-done((bf16[17,64,256]{2,1,0:T(8,128)(2,1)S(1)}, bf16[17,64,256]{2,1,0:T(8,128)(2,1)S(1)}, u32[]{:S(2)}, u32[]{:S(2)}) %collective-permute-start.3) | collective-permute-done | bytes 557088 | tf_op jit(solution)/shard_map/ppermute | solution.py:129
  29.0 0.0 copy-start
  29.0 0.6 %fusion.4.b_cols = s32[64]{0:T(128)} fusion(bf16[17,64,256]{2,1,0:T(8,128)(2,1)S(1)} %collective-permute-done.3.b_ref, s32[]{:T(128)} %bitcast.5), kind=kLoop, calls=%fused_computation.15 | loop fusion | flops 128 | bytes 388 | tf_op jit(solution)/shard_map/add | solution.py:132
  29.6 0.0 collective-permute-done.a_ref
  29.6 0.0 copy-start.1
  29.6 0.6 fusion.8.a_cols
  30.1 0.0 copy-done
  30.1 0.3 copy-done.1
  30.4 8.8 %shard_map.47 = (f32[16,64,256]{2,1,0:T(8,128)}, f32[16,64,256]{2,1,0:T(8,128)}) custom-call(s32[64]{0:T(128)} %fusion.8.a_cols, s32[64]{0:T(128)} %fusion.4.b_cols, s32[128]{0:T(128)} %reshape.125.want, bf16[17,64,256]{2,1,0:T(8,128)(2,1)} %copy-done.1, bf16[17,64,256]{2,1,0:T(8,128)(2,1)} %copy-done, ...), custom_call_target="tpu_custom_call", output_to_operand_aliasing={{0}: (5, {}), {1}: (6, {})} | custom-call | flops 268435456 | bytes 5308416 | tf_op jit(solution)/shard_map/pallas_call | solution.py:77
  39.3 15.0 %collective-permute-start.4 = (f32[16,64,256]{2,1,0:T(8,128)}, f32[16,64,256]{2,1,0:T(8,128)S(1)}, u32[]{:S(2)}, u32[]{:S(2)}) collective-permute-start(f32[16,64,256]{2,1,0:T(8,128)} %get-tuple-element.24), channel_id=1, source_target_pairs={{0,1},{1,0},{2,3},{3,2},{4,5},{5,4},{6,7},{7,6},{8,9},{9,8},{10,11... | collective-permute-start | bytes 3145736 | tf_op jit(solution)/shard_map/ppermute | solution.py:135
  54.2 2.5 %collective-permute-done.4 = f32[16,64,256]{2,1,0:T(8,128)S(1)} collective-permute-done((f32[16,64,256]{2,1,0:T(8,128)}, f32[16,64,256]{2,1,0:T(8,128)S(1)}, u32[]{:S(2)}, u32[]{:S(2)}) %collective-permute-start.4) | collective-permute-done | bytes 1048608 | tf_op jit(solution)/shard_map/ppermute | solution.py:135
  56.7 1.4 %add_bitcast_fusion = f32[16,64,1,256]{3,1,0,2:T(8,128)S(1)} fusion(f32[16,64,256]{2,1,0:T(8,128)} %get-tuple-element.23, f32[16,64,256]{2,1,0:T(8,128)S(1)} %collective-permute-done.4), kind=kLoop, calls=%fused_computation.2 | loop fusion | flops 262144 | bytes 3145728 | tf_op jit(solution)/shard_map/add | solution.py:136
  58.1 2.0 %copy.12 = f32[16,64,1,256]{3,2,1,0:T(1,128)} copy(f32[16,64,1,256]{3,1,0,2:T(8,128)S(1)} %add_bitcast_fusion) | data formatting | bytes 2097152 | tf_op jit(solution)/shard_map/add | solution.py:136
  (3 shorter events, 0.1 us)
Async XLA Ops:
  1.6 13.4 %copy-start.4 = (s32[16,1,8]{0,2,1:T(8,128)S(1)}, s32[16,1,8]{0,2,1:T(8,128)}, u32[]{:S(2)}) copy-start(s32[16,1,8]{0,2,1:T(8,128)} %param.9) | copy-start | bytes 1540
  2.8 12.9 %collective-permute-start.2 = (bf16[17,64,256]{2,1,0:T(8,128)(2,1)S(1)}, bf16[17,64,256]{2,1,0:T(8,128)(2,1)S(1)}, u32[]{:S(2)}, u32[]{:S(2)}) collective-permute-start(bf16[17,64,256]{2,1,0:T(8,128)(2,1)S(1)} %fusion.1), channel_id=1, source_target_pairs={{0,0},{5,1},{2,2},{7,3},{4,4},{1,5},{6,6},{3,7},{10,8},{15,9},{12,... | collective-permute-start | bytes 1671176 | tf_op jit(solution)/shard_map/ppermute | solution.py:129
  3.5 12.9 %collective-permute-start.1 = (bf16[17,64,256]{2,1,0:T(8,128)(2,1)S(1)}, bf16[17,64,256]{2,1,0:T(8,128)(2,1)S(1)}, u32[]{:S(2)}, u32[]{:S(2)}) collective-permute-start(bf16[17,64,256]{2,1,0:T(8,128)(2,1)S(1)} %fusion.1), channel_id=1, source_target_pairs={{0,0},{17,1},{10,2},{27,3},{20,4},{5,5},{30,6},{15,7},{8,8},{25,9}... | collective-permute-start | bytes 1671176 | tf_op jit(solution)/shard_map/ppermute | solution.py:128
  9.1 19.8 %collective-permute-start.3 = (bf16[17,64,256]{2,1,0:T(8,128)(2,1)S(1)}, bf16[17,64,256]{2,1,0:T(8,128)(2,1)S(1)}, u32[]{:S(2)}, u32[]{:S(2)}) collective-permute-start(bf16[17,64,256]{2,1,0:T(8,128)(2,1)S(1)} %fusion.1), channel_id=1, source_target_pairs={{2,0},{7,1},{4,2},{1,3},{6,4},{3,5},{0,6},{5,7},{12,8},{9,9},{14,1... | collective-permute-start | bytes 1671176 | tf_op jit(solution)/shard_map/ppermute | solution.py:129
  13.0 16.6 %collective-permute-start = (bf16[17,64,256]{2,1,0:T(8,128)(2,1)S(1)}, bf16[17,64,256]{2,1,0:T(8,128)(2,1)S(1)}, u32[]{:S(2)}, u32[]{:S(2)}) collective-permute-start(bf16[17,64,256]{2,1,0:T(8,128)(2,1)S(1)} %fusion.1), channel_id=1, source_target_pairs={{8,0},{25,1},{18,2},{3,3},{28,4},{13,5},{6,6},{23,7},{16,8},{1,9},... | collective-permute-start | bytes 1671176 | tf_op jit(solution)/shard_map/ppermute | solution.py:128
  15.7 1.2 %copy-start.2 = (bf16[17,64,256]{2,1,0:T(8,128)(2,1)}, bf16[17,64,256]{2,1,0:T(8,128)(2,1)S(1)}, u32[]{:S(2)}) copy-start(bf16[17,64,256]{2,1,0:T(8,128)(2,1)S(1)} %collective-permute-done.2.b_ref) | copy-start | bytes 1671172
  16.3 0.8 %copy-start.3 = (bf16[17,64,256]{2,1,0:T(8,128)(2,1)}, bf16[17,64,256]{2,1,0:T(8,128)(2,1)S(1)}, u32[]{:S(2)}) copy-start(bf16[17,64,256]{2,1,0:T(8,128)(2,1)S(1)} %collective-permute-done.1.a_ref) | copy-start | bytes 1671172
  29.0 1.2 %copy-start = (bf16[17,64,256]{2,1,0:T(8,128)(2,1)}, bf16[17,64,256]{2,1,0:T(8,128)(2,1)S(1)}, u32[]{:S(2)}) copy-start(bf16[17,64,256]{2,1,0:T(8,128)(2,1)S(1)} %collective-permute-done.3.b_ref) | copy-start | bytes 1671172
  29.6 0.8 %copy-start.1 = (bf16[17,64,256]{2,1,0:T(8,128)(2,1)}, bf16[17,64,256]{2,1,0:T(8,128)(2,1)S(1)}, u32[]{:S(2)}) copy-start(bf16[17,64,256]{2,1,0:T(8,128)(2,1)S(1)} %collective-permute-done.a_ref) | copy-start | bytes 1671172
  39.3 17.5 %collective-permute-start.4 = (f32[16,64,256]{2,1,0:T(8,128)}, f32[16,64,256]{2,1,0:T(8,128)S(1)}, u32[]{:S(2)}, u32[]{:S(2)}) collective-permute-start(f32[16,64,256]{2,1,0:T(8,128)} %get-tuple-element.24), channel_id=1, source_target_pairs={{0,1},{1,0},{2,3},{3,2},{4,5},{5,4},{6,7},{7,6},{8,9},{9,8},{10,11... | collective-permute-start | bytes 3145736 | tf_op jit(solution)/shard_map/ppermute | solution.py:135
where the time goes:
time: 60.5 us; the launch traced here: 60.1 us
  starting transfers between devices  27.1 us (45%)
  Pallas kernels  17 us (28%)
  other arithmetic  6.29 us (10%)
  local copies, waits for them, and re-layouts  4.67 us (8%)
  waiting for transfers between devices  4.4 us (7%)
  between operations  0.66 us (1%)
    pallas_call x2, Pallas kernels, one_step(): pl.pallas_call(step_kernel, in_specs=[smem] * 3 + [vmem] * (2 + len(sums)...  17 us
    ppermute x1, starting transfers between devices, per_device(): got = lax.ppermute(theirs, 'layer', [(0, 1), (1, 0)])  15 us
    ppermute x2, starting transfers between devices, per_device(): left = lax.ppermute(payload, ('row', 'col', 'layer'), left_pairs)  7.63 us
    ppermute x2, starting transfers between devices, per_device(): right = lax.ppermute(payload, ('row', 'col', 'layer'), right_pairs)  4.56 us
    ppermute x1, waiting for transfers between devices, per_device(): got = lax.ppermute(theirs, 'layer', [(0, 1), (1, 0)])  2.5 us
    add x1, local copies, waits for them, and re-layouts, per_device(): return mine[:, :, None, :] + got[:, :, None, :]  2.05 us
    ppermute x2, waiting for transfers between devices, per_device(): right = lax.ppermute(payload, ('row', 'col', 'layer'), right_pairs)  1.88 us
    add x1, other arithmetic, per_device(): return mine[:, :, None, :] + got[:, :, None, :]  1.36 us
  transfers between devices with their start and end apart: 5, of which 2 were waited for; matrix products, arithmetic and copies ran while one was open for 6% of the time, Pallas kernels for 14%

commit v1 on v0

--- a/solution.py
+++ b/solution.py
@@ -40,7 +40,7 @@
     for n in range(rows * slots):
         slot_of[(n // slots) * rows + b_cols[n]] = jnp.int32(n % slots)
 
-    def one_row(r, carry):
+    def one_row(r, sel_ref):
         for p in range(slots):
             k = a_cols[r * slots + p]
             for g in range(outs // 2):
@@ -57,9 +57,15 @@
         else:
             mine_ref[r] = mine_in[r] + prod[:, :half]
             theirs_ref[r] = theirs_in[r] + prod[:, half:]
+
+    group = sel_ref.shape[0]
+
+    def some_rows(n, carry):
+        for m in range(group):
+            one_row(group * n + m, sel_ref.at[m])
         return carry
 
-    lax.fori_loop(0, rows, one_row, 0)
+    lax.fori_loop(0, rows // group, some_rows, 0)
 
 
 def one_step(mine, theirs, left, right, a_cols, b_cols, want):
@@ -80,7 +86,7 @@
         out_specs=[vmem, vmem],
         scratch_shapes=[
             pltpu.VMEM((rows, seg // width + 1, 2, width, 2 * width), right.dtype),
-            pltpu.VMEM((seg, outs * width), right.dtype),
+            pltpu.VMEM((4 if rows % 4 == 0 else 1, seg, outs * width), right.dtype),
             pltpu.SMEM((rows * rows,), jnp.int32),
         ],
         out_shape=[jax.ShapeDtypeStruct((rows, width, share), jnp.float32)] * 2,

time: 60.5 us -> 57.5 us (0.950)
  Pallas kernels: 17 us -> 14 us
  waiting for transfers between devices: 4.4 us -> 5.88 us
  starting transfers between devices: 27.1 us -> 25.7 us
    pallas_call x2, Pallas kernels: 17 us -> 14 us  [one_step(): pl.pallas_call(step_kernel, in_specs=[smem] * 3 + [vmem] * (2 + len(sums)...]
    ppermute x2, waiting for transfers between devices: 1.88 us -> 3.37 us  [per_device(): right = lax.ppermute(payload, ('row', 'col', 'layer'), right_pairs)]
    ppermute x1, starting transfers between devices: 15 us -> 13.5 us  [per_device(): got = lax.ppermute(theirs, 'layer', [(0, 1), (1, 0)])]
  transfers between devices with their start and end apart: 5 -> 5, of which waited for: 2 -> 2; matrix products, arithmetic and copies ran while one was open for 6% -> 6% of each run, Pallas kernels for 14% -> 12%
where the time goes in v1:
time: 57.5 us; the launch traced here: 57.1 us
  starting transfers between devices  25.7 us (45%)
  Pallas kernels  14 us (24%)
  other arithmetic  6.29 us (11%)
  waiting for transfers between devices  5.88 us (10%)
  local copies, waits for them, and re-layouts  4.67 us (8%)
  between operations  0.66 us (1%)
    pallas_call x2, Pallas kernels, one_step(): pl.pallas_call(step_kernel, in_specs=[smem] * 3 + [vmem] * (2 + len(sums)...  14 us
    ppermute x1, starting transfers between devices, per_device(): got = lax.ppermute(theirs, 'layer', [(0, 1), (1, 0)])  13.5 us
    ppermute x2, starting transfers between devices, per_device(): left = lax.ppermute(payload, ('row', 'col', 'layer'), left_pairs)  7.63 us
    ppermute x2, starting transfers between devices, per_device(): right = lax.ppermute(payload, ('row', 'col', 'layer'), right_pairs)  4.56 us
    ppermute x2, waiting for transfers between devices, per_device(): right = lax.ppermute(payload, ('row', 'col', 'layer'), right_pairs)  3.37 us
    ppermute x1, waiting for transfers between devices, per_device(): got = lax.ppermute(theirs, 'layer', [(0, 1), (1, 0)])  2.5 us
    add x1, local copies, waits for them, and re-layouts, per_device(): return mine[:, :, None, :] + got[:, :, None, :]  2.05 us
    add x1, other arithmetic, per_device(): return mine[:, :, None, :] + got[:, :, None, :]  1.36 us
  transfers between devices with their start and end apart: 5, of which 2 were waited for; matrix products, arithmetic and copies ran while one was open for 6% of the time, Pallas kernels for 12%

profile of v1, /device:TPU:5, one launch (start us, length us, event | category | flops | bytes accessed | tf_op | source)
XLA Modules:
  0.0 57.1 jit_solution(3487252626111780340)
XLA Ops:
  0.0 0.7 %convert_element_type.35 = bf16[16,1,4]{0,2,1:T(4,128)(2,1)S(1)} convert(s32[16,1,4]{0,2,1:T(4,128)} %param.7) | non-fusion elementwise | flops 64 | bytes 384 | tf_op jit(solution)/shard_map/convert_element_type | solution.py:106
  0.7 0.1 copy.10
  0.8 0.1 convert_element_type.36
  0.9 0.7 %broadcast_compare_fusion = pred[16,256]{1,0:T(8,128)(4,1)S(1)} fusion(s32[256]{0:T(256)S(1)} %and_select_fusion, s32[16]{0:T(128)} %bitcast.24), kind=kLoop, calls=%fused_computation.7 | loop fusion | flops 4096 | bytes 5184 | tf_op jit(solution)/shard_map/lt | solution.py:103
  1.6 0.0 copy-start.4
  1.6 1.1 %bitcast_select_fusion = bf16[16,64,256]{2,1,0:T(8,128)(2,1)S(1)} fusion(bf16[16,64,1,256]{3,1,2,0:T(8,128)(2,1)} %param.6, pred[16,256]{1,0:T(8,128)(4,1)S(1)} %broadcast_compare_fusion), kind=kLoop, calls=%fused_computation.4 | loop fusion | flops 262144 | bytes 1052672 | tf_op jit(solution)/shard_map/jit(_where)/select_n | solution.py:103
  2.8 0.7 %collective-permute-start.2 = (bf16[17,64,256]{2,1,0:T(8,128)(2,1)S(1)}, bf16[17,64,256]{2,1,0:T(8,128)(2,1)S(1)}, u32[]{:S(2)}, u32[]{:S(2)}) collective-permute-start(bf16[17,64,256]{2,1,0:T(8,128)(2,1)S(1)} %fusion.1), channel_id=1, source_target_pairs={{0,0},{5,1},{2,2},{7,3},{4,4},{1,5},{6,6},{3,7},{10,8},{15,9},{12,... | collective-permute-start | bytes 1671176 | tf_op jit(solution)/shard_map/ppermute | solution.py:135
  3.5 5.7 %collective-permute-start.1 = (bf16[17,64,256]{2,1,0:T(8,128)(2,1)S(1)}, bf16[17,64,256]{2,1,0:T(8,128)(2,1)S(1)}, u32[]{:S(2)}, u32[]{:S(2)}) collective-permute-start(bf16[17,64,256]{2,1,0:T(8,128)(2,1)S(1)} %fusion.1), channel_id=1, source_target_pairs={{0,0},{17,1},{10,2},{27,3},{20,4},{5,5},{30,6},{15,7},{8,8},{25,9}... | collective-permute-start | bytes 1671176 | tf_op jit(solution)/shard_map/ppermute | solution.py:134
  9.1 3.9 %collective-permute-start.3 = (bf16[17,64,256]{2,1,0:T(8,128)(2,1)S(1)}, bf16[17,64,256]{2,1,0:T(8,128)(2,1)S(1)}, u32[]{:S(2)}, u32[]{:S(2)}) collective-permute-start(bf16[17,64,256]{2,1,0:T(8,128)(2,1)S(1)} %fusion.1), channel_id=1, source_target_pairs={{2,0},{7,1},{4,2},{1,3},{6,4},{3,5},{0,6},{5,7},{12,8},{9,9},{14,1... | collective-permute-start | bytes 1671176 | tf_op jit(solution)/shard_map/ppermute | solution.py:135
  13.0 2.0 %collective-permute-start = (bf16[17,64,256]{2,1,0:T(8,128)(2,1)S(1)}, bf16[17,64,256]{2,1,0:T(8,128)(2,1)S(1)}, u32[]{:S(2)}, u32[]{:S(2)}) collective-permute-start(bf16[17,64,256]{2,1,0:T(8,128)(2,1)S(1)} %fusion.1), channel_id=1, source_target_pairs={{8,0},{25,1},{18,2},{3,3},{28,4},{13,5},{6,6},{23,7},{16,8},{1,9},... | collective-permute-start | bytes 1671176 | tf_op jit(solution)/shard_map/ppermute | solution.py:134
  15.0 0.0 copy-done.4
  15.0 0.1 copy.11
  15.1 0.6 %reshape.125.want = s32[128]{0:T(128)} reshape(s32[16,8]{1,0:T(8,128)S(1)} %copy.11) | data formatting | bytes 1024 | tf_op jit(solution)/shard_map/reshape | solution.py:123
  15.7 0.0 collective-permute-done.2.b_ref
  15.7 0.0 copy-start.2
  15.7 0.6 %fusion.5.b_cols = s32[64]{0:T(128)} fusion(bf16[17,64,256]{2,1,0:T(8,128)(2,1)S(1)} %collective-permute-done.2.b_ref), kind=kLoop, calls=%fused_computation.17 | loop fusion | flops 64 | bytes 384 | tf_op jit(solution)/shard_map/convert_element_type | solution.py:138
  16.3 0.0 collective-permute-done.1.a_ref
  16.3 0.0 copy-start.3
  16.3 0.6 fusion.6.a_cols
  16.9 0.0 copy-done.2
  16.9 0.3 copy-done.3
  17.2 6.6 %shard_map.46 = (f32[16,64,256]{2,1,0:T(8,128)}, f32[16,64,256]{2,1,0:T(8,128)}) custom-call(s32[64]{0:T(128)} %fusion.6.a_cols, s32[64]{0:T(128)} %fusion.5.b_cols, s32[128]{0:T(128)} %reshape.125.want, bf16[17,64,256]{2,1,0:T(8,128)(2,1)} %copy-done.3, bf16[17,64,256]{2,1,0:T(8,128)(2,1)} %copy-done.2), custom_call_target="tpu_custom_call" | custom-call | flops 268435456 | bytes 3211264 | tf_op jit(solution)/shard_map/pallas_call | solution.py:83
  23.8 1.2 %slice.39 = f32[1,1,1]{2,1,0:T(1,128)} slice(f32[16,64,256]{2,1,0:T(8,128)} %get-tuple-element.21.refs_0_), slice={[0:1], [0:1], [0:1]} | slice | bytes 8 | tf_op jit(solution)/shard_map/slice | solution.py:136
  25.6 3.4 %collective-permute-done.3.b_ref = bf16[17,64,256]{2,1,0:T(8,128)(2,1)S(1)} collective-permute-done((bf16[17,64,256]{2,1,0:T(8,128)(2,1)S(1)}, bf16[17,64,256]{2,1,0:T(8,128)(2,1)S(1)}, u32[]{:S(2)}, u32[]{:S(2)}) %collective-permute-start.3) | collective-permute-done | bytes 557088 | tf_op jit(solution)/shard_map/ppermute | solution.py:135
  29.0 0.0 copy-start
  29.0 0.6 %fusion.4.b_cols = s32[64]{0:T(128)} fusion(bf16[17,64,256]{2,1,0:T(8,128)(2,1)S(1)} %collective-permute-done.3.b_ref, s32[]{:T(128)} %bitcast.5), kind=kLoop, calls=%fused_computation.15 | loop fusion | flops 128 | bytes 388 | tf_op jit(solution)/shard_map/add | solution.py:138
  29.6 0.0 collective-permute-done.a_ref
  29.6 0.0 copy-start.1
  29.6 0.6 fusion.8.a_cols
  30.1 0.0 copy-done
  30.1 0.3 copy-done.1
  30.4 7.3 %shard_map.47 = (f32[16,64,256]{2,1,0:T(8,128)}, f32[16,64,256]{2,1,0:T(8,128)}) custom-call(s32[64]{0:T(128)} %fusion.8.a_cols, s32[64]{0:T(128)} %fusion.4.b_cols, s32[128]{0:T(128)} %reshape.125.want, bf16[17,64,256]{2,1,0:T(8,128)(2,1)} %copy-done.1, bf16[17,64,256]{2,1,0:T(8,128)(2,1)} %copy-done, ...), custom_call_target="tpu_custom_call", output_to_operand_aliasing={{0}: (5, {}), {1}: (6, {})} | custom-call | flops 268435456 | bytes 5308416 | tf_op jit(solution)/shard_map/pallas_call | solution.py:83
  37.8 13.5 %collective-permute-start.4 = (f32[16,64,256]{2,1,0:T(8,128)}, f32[16,64,256]{2,1,0:T(8,128)S(1)}, u32[]{:S(2)}, u32[]{:S(2)}) collective-permute-start(f32[16,64,256]{2,1,0:T(8,128)} %get-tuple-element.24), channel_id=1, source_target_pairs={{0,1},{1,0},{2,3},{3,2},{4,5},{5,4},{6,7},{7,6},{8,9},{9,8},{10,11... | collective-permute-start | bytes 3145736 | tf_op jit(solution)/shard_map/ppermute | solution.py:141
  51.2 2.5 %collective-permute-done.4 = f32[16,64,256]{2,1,0:T(8,128)S(1)} collective-permute-done((f32[16,64,256]{2,1,0:T(8,128)}, f32[16,64,256]{2,1,0:T(8,128)S(1)}, u32[]{:S(2)}, u32[]{:S(2)}) %collective-permute-start.4) | collective-permute-done | bytes 1048608 | tf_op jit(solution)/shard_map/ppermute | solution.py:141
  53.7 1.4 %add_bitcast_fusion = f32[16,64,1,256]{3,1,0,2:T(8,128)S(1)} fusion(f32[16,64,256]{2,1,0:T(8,128)} %get-tuple-element.23, f32[16,64,256]{2,1,0:T(8,128)S(1)} %collective-permute-done.4), kind=kLoop, calls=%fused_computation.2 | loop fusion | flops 262144 | bytes 3145728 | tf_op jit(solution)/shard_map/add | solution.py:142
  55.1 2.0 %copy.12 = f32[16,64,1,256]{3,2,1,0:T(1,128)} copy(f32[16,64,1,256]{3,1,0,2:T(8,128)S(1)} %add_bitcast_fusion) | data formatting | bytes 2097152 | tf_op jit(solution)/shard_map/add | solution.py:142
  (3 shorter events, 0.1 us)
Async XLA Ops:
  1.6 13.4 %copy-start.4 = (s32[16,1,8]{0,2,1:T(8,128)S(1)}, s32[16,1,8]{0,2,1:T(8,128)}, u32[]{:S(2)}) copy-start(s32[16,1,8]{0,2,1:T(8,128)} %param.9) | copy-start | bytes 1540
  2.8 12.9 %collective-permute-start.2 = (bf16[17,64,256]{2,1,0:T(8,128)(2,1)S(1)}, bf16[17,64,256]{2,1,0:T(8,128)(2,1)S(1)}, u32[]{:S(2)}, u32[]{:S(2)}) collective-permute-start(bf16[17,64,256]{2,1,0:T(8,128)(2,1)S(1)} %fusion.1), channel_id=1, source_target_pairs={{0,0},{5,1},{2,2},{7,3},{4,4},{1,5},{6,6},{3,7},{10,8},{15,9},{12,... | collective-permute-start | bytes 1671176 | tf_op jit(solution)/shard_map/ppermute | solution.py:135
  3.5 12.9 %collective-permute-start.1 = (bf16[17,64,256]{2,1,0:T(8,128)(2,1)S(1)}, bf16[17,64,256]{2,1,0:T(8,128)(2,1)S(1)}, u32[]{:S(2)}, u32[]{:S(2)}) collective-permute-start(bf16[17,64,256]{2,1,0:T(8,128)(2,1)S(1)} %fusion.1), channel_id=1, source_target_pairs={{0,0},{17,1},{10,2},{27,3},{20,4},{5,5},{30,6},{15,7},{8,8},{25,9}... | collective-permute-start | bytes 1671176 | tf_op jit(solution)/shard_map/ppermute | solution.py:134
  9.1 19.8 %collective-permute-start.3 = (bf16[17,64,256]{2,1,0:T(8,128)(2,1)S(1)}, bf16[17,64,256]{2,1,0:T(8,128)(2,1)S(1)}, u32[]{:S(2)}, u32[]{:S(2)}) collective-permute-start(bf16[17,64,256]{2,1,0:T(8,128)(2,1)S(1)} %fusion.1), channel_id=1, source_target_pairs={{2,0},{7,1},{4,2},{1,3},{6,4},{3,5},{0,6},{5,7},{12,8},{9,9},{14,1... | collective-permute-start | bytes 1671176 | tf_op jit(solution)/shard_map/ppermute | solution.py:135
  13.0 16.6 %collective-permute-start = (bf16[17,64,256]{2,1,0:T(8,128)(2,1)S(1)}, bf16[17,64,256]{2,1,0:T(8,128)(2,1)S(1)}, u32[]{:S(2)}, u32[]{:S(2)}) collective-permute-start(bf16[17,64,256]{2,1,0:T(8,128)(2,1)S(1)} %fusion.1), channel_id=1, source_target_pairs={{8,0},{25,1},{18,2},{3,3},{28,4},{13,5},{6,6},{23,7},{16,8},{1,9},... | collective-permute-start | bytes 1671176 | tf_op jit(solution)/shard_map/ppermute | solution.py:134
  15.7 1.2 %copy-start.2 = (bf16[17,64,256]{2,1,0:T(8,128)(2,1)}, bf16[17,64,256]{2,1,0:T(8,128)(2,1)S(1)}, u32[]{:S(2)}) copy-start(bf16[17,64,256]{2,1,0:T(8,128)(2,1)S(1)} %collective-permute-done.2.b_ref) | copy-start | bytes 1671172
  16.3 0.8 %copy-start.3 = (bf16[17,64,256]{2,1,0:T(8,128)(2,1)}, bf16[17,64,256]{2,1,0:T(8,128)(2,1)S(1)}, u32[]{:S(2)}) copy-start(bf16[17,64,256]{2,1,0:T(8,128)(2,1)S(1)} %collective-permute-done.1.a_ref) | copy-start | bytes 1671172
  29.0 1.2 %copy-start = (bf16[17,64,256]{2,1,0:T(8,128)(2,1)}, bf16[17,64,256]{2,1,0:T(8,128)(2,1)S(1)}, u32[]{:S(2)}) copy-start(bf16[17,64,256]{2,1,0:T(8,128)(2,1)S(1)} %collective-permute-done.3.b_ref) | copy-start | bytes 1671172
  29.6 0.8 %copy-start.1 = (bf16[17,64,256]{2,1,0:T(8,128)(2,1)}, bf16[17,64,256]{2,1,0:T(8,128)(2,1)S(1)}, u32[]{:S(2)}) copy-start(bf16[17,64,256]{2,1,0:T(8,128)(2,1)S(1)} %collective-permute-done.a_ref) | copy-start | bytes 1671172
  37.8 16.0 %collective-permute-start.4 = (f32[16,64,256]{2,1,0:T(8,128)}, f32[16,64,256]{2,1,0:T(8,128)S(1)}, u32[]{:S(2)}, u32[]{:S(2)}) collective-permute-start(f32[16,64,256]{2,1,0:T(8,128)} %get-tuple-element.24), channel_id=1, source_target_pairs={{0,1},{1,0},{2,3},{3,2},{4,5},{5,4},{6,7},{7,6},{8,9},{9,8},{10,11... | collective-permute-start | bytes 3145736 | tf_op jit(solution)/shard_map/ppermute | solution.py:141

commit v2 on v1

--- a/solution.py
+++ b/solution.py
@@ -9,11 +9,11 @@
 
 
 def step_kernel(a_cols, b_cols, want, a_ref, b_ref, *refs):
-    if len(refs) == 7:
-        mine_in, theirs_in, mine_ref, theirs_ref, place_ref, sel_ref, slot_of = refs
+    if len(refs) == 8:
+        mine_in, theirs_in, mine_ref, theirs_ref, tick, place_ref, sel_ref, slot_of = refs
     else:
         mine_in = theirs_in = None
-        mine_ref, theirs_ref, place_ref, sel_ref, slot_of = refs
+        mine_ref, theirs_ref, tick, place_ref, sel_ref, slot_of = refs
     width = a_ref.shape[1]
     seg = a_ref.shape[2]
     slots = seg // width
@@ -21,6 +21,7 @@
     outs = want.shape[0] // rows
     lane = lax.broadcasted_iota(jnp.int32, (width, 2 * width), 1)
     zero = jnp.zeros((width, 2 * width), b_ref.dtype)
+    tick[0] = jnp.int32(0)
 
     def fill(k, carry):
         for q in range(slots):
@@ -83,13 +84,14 @@
     return pl.pallas_call(
         step_kernel,
         in_specs=[smem] * 3 + [vmem] * (2 + len(sums)),
-        out_specs=[vmem, vmem],
+        out_specs=[vmem, vmem, smem],
         scratch_shapes=[
             pltpu.VMEM((rows, seg // width + 1, 2, width, 2 * width), right.dtype),
             pltpu.VMEM((4 if rows % 4 == 0 else 1, seg, outs * width), right.dtype),
             pltpu.SMEM((rows * rows,), jnp.int32),
         ],
-        out_shape=[jax.ShapeDtypeStruct((rows, width, share), jnp.float32)] * 2,
+        out_shape=[jax.ShapeDtypeStruct((rows, width, share), jnp.float32)] * 2
+        + [jax.ShapeDtypeStruct((1,), jnp.int32)],
         input_output_aliases={5: 0, 6: 1} if sums else {},
         cost_estimate=cost,
     )(a_cols, b_cols, want, left, right, *sums)
@@ -122,6 +124,7 @@
     both = jnp.concatenate([out_cols[:, 0, :], out_cols[:, 0, :]], axis=1)
     want = lax.dynamic_slice_in_dim(both, me_l * share, outs, axis=1).reshape(-1)
     mine = theirs = None
+    tick = jnp.zeros((1,), jnp.int32)
     for s in range(steps):
         left_pairs = []
         right_pairs = []
@@ -133,10 +136,10 @@
                     right_pairs.append((flat(r, t, l), flat(r, c, l)))
         left = lax.ppermute(payload, ("row", "col", "layer"), left_pairs)
         right = lax.ppermute(payload, ("row", "col", "layer"), right_pairs)
-        after = 0 if mine is None else (mine[0, 0, 0] * 0).astype(jnp.int32)
-        a_cols = left[row_count, 0, :columns.shape[0]].astype(jnp.int32) + after
-        b_cols = right[row_count, 0, :columns.shape[0]].astype(jnp.int32) + after
-        mine, theirs = one_step(mine, theirs, left, right, a_cols, b_cols, want)
+        n = columns.shape[0]
+        a_cols = left[row_count, 0, :n].astype(jnp.int32) + tick
+        b_cols = right[row_count, 0, :n].astype(jnp.int32) + tick
+        mine, theirs, tick = one_step(mine, theirs, left, right, a_cols, b_cols, want)
 
     got = lax.ppermute(theirs, "layer", [(0, 1), (1, 0)])
     return mine[:, :, None, :] + got[:, :, None, :]

time: 57.5 us -> 56.6 us (0.984)
  waiting for transfers between devices: 5.88 us -> 7.69 us
  starting transfers between devices: 25.7 us -> 23.9 us
  local copies, waits for them, and re-layouts: 4.67 us -> 3.12 us
  other arithmetic: 6.29 us -> 7.47 us
    ppermute x1, starting transfers between devices: 13.5 us -> 11.7 us  [per_device(): got = lax.ppermute(theirs, 'layer', [(0, 1), (1, 0)])]
    ppermute x2, waiting for transfers between devices: 3.37 us -> 5.11 us  [per_device(): right = lax.ppermute(payload, ('row', 'col', 'layer'), right_pairs)]
    slice x1 -> x0, local copies, waits for them, and re-layouts: 1.19 us -> none  [per_device(): after = 0 if mine is None else (mine[0, 0, 0] * 0).astype(jnp.int32)]
    add x2, other arithmetic: 1.18 us -> 2.35 us  [the longest x1 1.22 us: per_device(): a_cols = left[row_count, 0, :n].astype(jnp.int32) + tick]
  transfers between devices with their start and end apart: 5 -> 5, of which waited for: 2 -> 3; matrix products, arithmetic and copies ran while one was open for 6% -> 5% of each run, Pallas kernels for 12% -> 12%
where the time goes in v2:
time: 56.6 us; the launch traced here: 56.3 us
  starting transfers between devices  23.9 us (42%)
  Pallas kernels  14 us (25%)
  waiting for transfers between devices  7.69 us (14%)
  other arithmetic  7.47 us (13%)
  local copies, waits for them, and re-layouts  3.12 us (6%)
    pallas_call x2, Pallas kernels, one_step(): pl.pallas_call(step_kernel, in_specs=[smem] * 3 + [vmem] * (2 + len(sums)...  14 us
    ppermute x1, starting transfers between devices, per_device(): got = lax.ppermute(theirs, 'layer', [(0, 1), (1, 0)])  11.7 us
    ppermute x2, starting transfers between devices, per_device(): left = lax.ppermute(payload, ('row', 'col', 'layer'), left_pairs)  7.63 us
    ppermute x2, waiting for transfers between devices, per_device(): right = lax.ppermute(payload, ('row', 'col', 'layer'), right_pairs)  5.11 us
    ppermute x2, starting transfers between devices, per_device(): right = lax.ppermute(payload, ('row', 'col', 'layer'), right_pairs)  4.56 us
    ppermute x1, waiting for transfers between devices, per_device(): got = lax.ppermute(theirs, 'layer', [(0, 1), (1, 0)])  2.5 us
    add x1, local copies, waits for them, and re-layouts, per_device(): return mine[:, :, None, :] + got[:, :, None, :]  2.05 us
    add x1, other arithmetic, per_device(): return mine[:, :, None, :] + got[:, :, None, :]  1.36 us
  transfers between devices with their start and end apart: 5, of which 3 were waited for; matrix products, arithmetic and copies ran while one was open for 5% of the time, Pallas kernels for 12%

profile of v2, /device:TPU:5, one launch (start us, length us, event | category | flops | bytes accessed | tf_op | source)
XLA Modules:
  0.0 56.3 jit_solution(16547652871727566827)
XLA Ops:
  0.0 0.7 %convert_element_type.29 = bf16[16,1,4]{0,2,1:T(4,128)(2,1)S(1)} convert(s32[16,1,4]{0,2,1:T(4,128)} %param.7) | non-fusion elementwise | flops 64 | bytes 384 | tf_op jit(solution)/shard_map/convert_element_type | solution.py:108
  0.7 0.1 copy.10
  0.8 0.1 convert_element_type.30
  0.9 0.7 %broadcast_compare_fusion = pred[16,256]{1,0:T(8,128)(4,1)S(1)} fusion(s32[256]{0:T(256)S(1)} %and_select_fusion, s32[16]{0:T(128)} %bitcast.24), kind=kLoop, calls=%fused_computation.7 | loop fusion | flops 4096 | bytes 5184 | tf_op jit(solution)/shard_map/lt | solution.py:105
  1.6 0.0 copy-start.4
  1.6 1.1 %bitcast_select_fusion = bf16[16,64,256]{2,1,0:T(8,128)(2,1)S(1)} fusion(bf16[16,64,1,256]{3,1,2,0:T(8,128)(2,1)} %param.6, pred[16,256]{1,0:T(8,128)(4,1)S(1)} %broadcast_compare_fusion), kind=kLoop, calls=%fused_computation.4 | loop fusion | flops 262144 | bytes 1052672 | tf_op jit(solution)/shard_map/jit(_where)/select_n | solution.py:105
  2.8 0.7 %collective-permute-start.2 = (bf16[17,64,256]{2,1,0:T(8,128)(2,1)S(1)}, bf16[17,64,256]{2,1,0:T(8,128)(2,1)S(1)}, u32[]{:S(2)}, u32[]{:S(2)}) collective-permute-start(bf16[17,64,256]{2,1,0:T(8,128)(2,1)S(1)} %fusion.1), channel_id=1, source_target_pairs={{0,0},{5,1},{2,2},{7,3},{4,4},{1,5},{6,6},{3,7},{10,8},{15,9},{12,... | collective-permute-start | bytes 1671176 | tf_op jit(solution)/shard_map/ppermute | solution.py:138
  3.5 5.7 %collective-permute-start.1 = (bf16[17,64,256]{2,1,0:T(8,128)(2,1)S(1)}, bf16[17,64,256]{2,1,0:T(8,128)(2,1)S(1)}, u32[]{:S(2)}, u32[]{:S(2)}) collective-permute-start(bf16[17,64,256]{2,1,0:T(8,128)(2,1)S(1)} %fusion.1), channel_id=1, source_target_pairs={{0,0},{17,1},{10,2},{27,3},{20,4},{5,5},{30,6},{15,7},{8,8},{25,9}... | collective-permute-start | bytes 1671176 | tf_op jit(solution)/shard_map/ppermute | solution.py:137
  9.1 3.9 %collective-permute-start.3 = (bf16[17,64,256]{2,1,0:T(8,128)(2,1)S(1)}, bf16[17,64,256]{2,1,0:T(8,128)(2,1)S(1)}, u32[]{:S(2)}, u32[]{:S(2)}) collective-permute-start(bf16[17,64,256]{2,1,0:T(8,128)(2,1)S(1)} %fusion.1), channel_id=1, source_target_pairs={{2,0},{7,1},{4,2},{1,3},{6,4},{3,5},{0,6},{5,7},{12,8},{9,9},{14,1... | collective-permute-start | bytes 1671176 | tf_op jit(solution)/shard_map/ppermute | solution.py:138
  13.0 2.0 %collective-permute-start = (bf16[17,64,256]{2,1,0:T(8,128)(2,1)S(1)}, bf16[17,64,256]{2,1,0:T(8,128)(2,1)S(1)}, u32[]{:S(2)}, u32[]{:S(2)}) collective-permute-start(bf16[17,64,256]{2,1,0:T(8,128)(2,1)S(1)} %fusion.1), channel_id=1, source_target_pairs={{8,0},{25,1},{18,2},{3,3},{28,4},{13,5},{6,6},{23,7},{16,8},{1,9},... | collective-permute-start | bytes 1671176 | tf_op jit(solution)/shard_map/ppermute | solution.py:137
  15.0 0.0 copy-done.4
  15.0 0.1 copy.11
  15.1 0.6 %reshape.122.want = s32[128]{0:T(128)} reshape(s32[16,8]{1,0:T(8,128)S(1)} %copy.11) | data formatting | bytes 1024 | tf_op jit(solution)/shard_map/reshape | solution.py:125
  15.7 0.0 collective-permute-done.2.b_ref
  15.7 0.0 copy-start.2
  15.7 0.5 fusion.5.b_cols
  16.3 0.1 collective-permute-done.1.a_ref
  16.3 0.0 copy-start.3
  16.3 0.6 %fusion.6.a_cols = s32[64]{0:T(128)} fusion(bf16[17,64,256]{2,1,0:T(8,128)(2,1)S(1)} %collective-permute-done.1.a_ref), kind=kLoop, calls=%fused_computation.19 | loop fusion | flops 64 | bytes 384 | tf_op jit(solution)/shard_map/convert_element_type | solution.py:140
  17.0 0.0 copy-done.2
  17.0 0.2 copy-done.3
  17.2 6.7 %shard_map.46 = (f32[16,64,256]{2,1,0:T(8,128)}, f32[16,64,256]{2,1,0:T(8,128)}, s32[1]{0:T(128)}) custom-call(s32[64]{0:T(128)} %fusion.6.a_cols, s32[64]{0:T(128)} %fusion.5.b_cols, s32[128]{0:T(128)} %reshape.122.want, bf16[17,64,256]{2,1,0:T(8,128)(2,1)} %copy-done.3, bf16[17,64,256]{2,1,0:T(8,128)(2,1)} %copy-done.2), custom_call_target="tpu_custom_call" | custom-call | flops 268435456 | bytes 3211264 | tf_op jit(solution)/shard_map/pallas_call | solution.py:84
  23.9 5.1 %collective-permute-done.3.b_ref = bf16[17,64,256]{2,1,0:T(8,128)(2,1)S(1)} collective-permute-done((bf16[17,64,256]{2,1,0:T(8,128)(2,1)S(1)}, bf16[17,64,256]{2,1,0:T(8,128)(2,1)S(1)}, u32[]{:S(2)}, u32[]{:S(2)}) %collective-permute-start.3) | collective-permute-done | bytes 557088 | tf_op jit(solution)/shard_map/ppermute | solution.py:138
  29.0 0.0 copy-start
  29.0 1.1 %fusion.4.b_cols = s32[64]{0:T(128)} fusion(bf16[17,64,256]{2,1,0:T(8,128)(2,1)S(1)} %collective-permute-done.3.b_ref, s32[]{:T(128)} %bitcast.5), kind=kLoop, calls=%fused_computation.15 | loop fusion | flops 128 | bytes 388 | tf_op jit(solution)/shard_map/add | solution.py:141
  30.1 0.0 collective-permute-done.a_ref
  30.1 0.0 copy-start.1
  30.1 1.2 %fusion.8.a_cols = s32[64]{0:T(128)} fusion(bf16[17,64,256]{2,1,0:T(8,128)(2,1)S(1)} %collective-permute-done.a_ref, s32[]{:T(128)} %bitcast.5), kind=kLoop, calls=%fused_computation.22 | loop fusion | flops 128 | bytes 388 | tf_op jit(solution)/shard_map/add | solution.py:140
  31.3 0.0 copy-done
  31.3 0.0 copy-done.1
  31.3 7.4 %shard_map.47 = (f32[16,64,256]{2,1,0:T(8,128)}, f32[16,64,256]{2,1,0:T(8,128)}, s32[1]{0:T(128)}) custom-call(s32[64]{0:T(128)} %fusion.8.a_cols, s32[64]{0:T(128)} %fusion.4.b_cols, s32[128]{0:T(128)} %reshape.122.want, bf16[17,64,256]{2,1,0:T(8,128)(2,1)} %copy-done.1, ...), custom_call_target="tpu_custom_call", output_to_operand_aliasing={{0}: (5, {}), {1}: (6, {})} | custom-call | flops 268435456 | bytes 5308416 | tf_op jit(solution)/shard_map/pallas_call | solution.py:84
  38.7 11.7 %collective-permute-start.4 = (f32[16,64,256]{2,1,0:T(8,128)}, f32[16,64,256]{2,1,0:T(8,128)S(1)}, u32[]{:S(2)}, u32[]{:S(2)}) collective-permute-start(f32[16,64,256]{2,1,0:T(8,128)} %get-tuple-element.26), channel_id=1, source_target_pairs={{0,1},{1,0},{2,3},{3,2},{4,5},{5,4},{6,7},{7,6},{8,9},{9,8},{10,11... | collective-permute-start | bytes 3145736 | tf_op jit(solution)/shard_map/ppermute | solution.py:144
  50.4 2.5 %collective-permute-done.4 = f32[16,64,256]{2,1,0:T(8,128)S(1)} collective-permute-done((f32[16,64,256]{2,1,0:T(8,128)}, f32[16,64,256]{2,1,0:T(8,128)S(1)}, u32[]{:S(2)}, u32[]{:S(2)}) %collective-permute-start.4) | collective-permute-done | bytes 1048608 | tf_op jit(solution)/shard_map/ppermute | solution.py:144
  52.9 1.4 %add_bitcast_fusion = f32[16,64,1,256]{3,1,0,2:T(8,128)S(1)} fusion(f32[16,64,256]{2,1,0:T(8,128)} %get-tuple-element.25, f32[16,64,256]{2,1,0:T(8,128)S(1)} %collective-permute-done.4), kind=kLoop, calls=%fused_computation.2 | loop fusion | flops 262144 | bytes 3145728 | tf_op jit(solution)/shard_map/add | solution.py:145
  54.2 2.0 %copy.12 = f32[16,64,1,256]{3,2,1,0:T(1,128)} copy(f32[16,64,1,256]{3,1,0,2:T(8,128)S(1)} %add_bitcast_fusion) | data formatting | bytes 2097152 | tf_op jit(solution)/shard_map/add | solution.py:145
  (3 shorter events, 0.1 us)
Async XLA Ops:
  1.6 13.4 %copy-start.4 = (s32[16,1,8]{0,2,1:T(8,128)S(1)}, s32[16,1,8]{0,2,1:T(8,128)}, u32[]{:S(2)}) copy-start(s32[16,1,8]{0,2,1:T(8,128)} %param.9) | copy-start | bytes 1540
  2.8 12.9 %collective-permute-start.2 = (bf16[17,64,256]{2,1,0:T(8,128)(2,1)S(1)}, bf16[17,64,256]{2,1,0:T(8,128)(2,1)S(1)}, u32[]{:S(2)}, u32[]{:S(2)}) collective-permute-start(bf16[17,64,256]{2,1,0:T(8,128)(2,1)S(1)} %fusion.1), channel_id=1, source_target_pairs={{0,0},{5,1},{2,2},{7,3},{4,4},{1,5},{6,6},{3,7},{10,8},{15,9},{12,... | collective-permute-start | bytes 1671176 | tf_op jit(solution)/shard_map/ppermute | solution.py:138
  3.5 12.9 %collective-permute-start.1 = (bf16[17,64,256]{2,1,0:T(8,128)(2,1)S(1)}, bf16[17,64,256]{2,1,0:T(8,128)(2,1)S(1)}, u32[]{:S(2)}, u32[]{:S(2)}) collective-permute-start(bf16[17,64,256]{2,1,0:T(8,128)(2,1)S(1)} %fusion.1), channel_id=1, source_target_pairs={{0,0},{17,1},{10,2},{27,3},{20,4},{5,5},{30,6},{15,7},{8,8},{25,9}... | collective-permute-start | bytes 1671176 | tf_op jit(solution)/shard_map/ppermute | solution.py:137
  9.1 19.8 %collective-permute-start.3 = (bf16[17,64,256]{2,1,0:T(8,128)(2,1)S(1)}, bf16[17,64,256]{2,1,0:T(8,128)(2,1)S(1)}, u32[]{:S(2)}, u32[]{:S(2)}) collective-permute-start(bf16[17,64,256]{2,1,0:T(8,128)(2,1)S(1)} %fusion.1), channel_id=1, source_target_pairs={{2,0},{7,1},{4,2},{1,3},{6,4},{3,5},{0,6},{5,7},{12,8},{9,9},{14,1... | collective-permute-start | bytes 1671176 | tf_op jit(solution)/shard_map/ppermute | solution.py:138
  13.0 17.1 %collective-permute-start = (bf16[17,64,256]{2,1,0:T(8,128)(2,1)S(1)}, bf16[17,64,256]{2,1,0:T(8,128)(2,1)S(1)}, u32[]{:S(2)}, u32[]{:S(2)}) collective-permute-start(bf16[17,64,256]{2,1,0:T(8,128)(2,1)S(1)} %fusion.1), channel_id=1, source_target_pairs={{8,0},{25,1},{18,2},{3,3},{28,4},{13,5},{6,6},{23,7},{16,8},{1,9},... | collective-permute-start | bytes 1671176 | tf_op jit(solution)/shard_map/ppermute | solution.py:137
  15.7 1.3 %copy-start.2 = (bf16[17,64,256]{2,1,0:T(8,128)(2,1)}, bf16[17,64,256]{2,1,0:T(8,128)(2,1)S(1)}, u32[]{:S(2)}) copy-start(bf16[17,64,256]{2,1,0:T(8,128)(2,1)S(1)} %collective-permute-done.2.b_ref) | copy-start | bytes 1671172
  16.3 0.8 %copy-start.3 = (bf16[17,64,256]{2,1,0:T(8,128)(2,1)}, bf16[17,64,256]{2,1,0:T(8,128)(2,1)S(1)}, u32[]{:S(2)}) copy-start(bf16[17,64,256]{2,1,0:T(8,128)(2,1)S(1)} %collective-permute-done.1.a_ref) | copy-start | bytes 1671172
  29.0 2.4 %copy-start = (bf16[17,64,256]{2,1,0:T(8,128)(2,1)}, bf16[17,64,256]{2,1,0:T(8,128)(2,1)S(1)}, u32[]{:S(2)}) copy-start(bf16[17,64,256]{2,1,0:T(8,128)(2,1)S(1)} %collective-permute-done.3.b_ref) | copy-start | bytes 1671172
  30.1 1.2 %copy-start.1 = (bf16[17,64,256]{2,1,0:T(8,128)(2,1)}, bf16[17,64,256]{2,1,0:T(8,128)(2,1)S(1)}, u32[]{:S(2)}) copy-start(bf16[17,64,256]{2,1,0:T(8,128)(2,1)S(1)} %collective-permute-done.a_ref) | copy-start | bytes 1671172
  38.7 14.2 %collective-permute-start.4 = (f32[16,64,256]{2,1,0:T(8,128)}, f32[16,64,256]{2,1,0:T(8,128)S(1)}, u32[]{:S(2)}, u32[]{:S(2)}) collective-permute-start(f32[16,64,256]{2,1,0:T(8,128)} %get-tuple-element.26), channel_id=1, source_target_pairs={{0,1},{1,0},{2,3},{3,2},{4,5},{5,4},{6,7},{7,6},{8,9},{9,8},{10,11... | collective-permute-start | bytes 3145736 | tf_op jit(solution)/shard_map/ppermute | solution.py:144

commit v3 on v2

--- a/solution.py
+++ b/solution.py
@@ -131,7 +131,7 @@
         for r in range(rows_n):
             for c in range(cols_n):
                 for l in range(layers):
-                    t = (r + c + s + l * steps) % rows_n
+                    t = r ^ c ^ (s + l * steps)
                     left_pairs.append((flat(t, c, l), flat(r, c, l)))
                     right_pairs.append((flat(r, t, l), flat(r, c, l)))
         left = lax.ppermute(payload, ("row", "col", "layer"), left_pairs)

time: 56.6 us -> 51.3 us (0.906)
  the two profiles are of different devices: /device:TPU:5 before, /device:TPU:0 now
where the time goes in v3:
time: 51.3 us; the launch traced here: 51 us
  starting transfers between devices  16.2 us (32%)
  Pallas kernels  14 us (27%)
  waiting for transfers between devices  10.1 us (20%)
  other arithmetic  7.47 us (15%)
  local copies, waits for them, and re-layouts  3.12 us (6%)
    pallas_call x2, Pallas kernels, one_step(): pl.pallas_call(step_kernel, in_specs=[smem] * 3 + [vmem] * (2 + len(sums)...  14 us
    ppermute x2, starting transfers between devices, per_device(): right = lax.ppermute(payload, ('row', 'col', 'layer'), right_pairs)  9.99 us
    ppermute x2, waiting for transfers between devices, per_device(): right = lax.ppermute(payload, ('row', 'col', 'layer'), right_pairs)  7.58 us
    ppermute x1, starting transfers between devices, per_device(): got = lax.ppermute(theirs, 'layer', [(0, 1), (1, 0)])  3.61 us
    ppermute x2, starting transfers between devices, per_device(): left = lax.ppermute(payload, ('row', 'col', 'layer'), left_pairs)  2.62 us
    ppermute x1, waiting for transfers between devices, per_device(): got = lax.ppermute(theirs, 'layer', [(0, 1), (1, 0)])  2.5 us
    add x1, local copies, waits for them, and re-layouts, per_device(): return mine[:, :, None, :] + got[:, :, None, :]  2.05 us
    add x1, other arithmetic, per_device(): return mine[:, :, None, :] + got[:, :, None, :]  1.36 us
  transfers between devices with their start and end apart: 5, of which 2 were waited for; matrix products, arithmetic and copies ran while one was open for 6% of the time, Pallas kernels for 13%

profile of v3, /device:TPU:0, one launch (start us, length us, event | category | flops | bytes accessed | tf_op | source)
XLA Modules:
  0.0 51.0 jit_solution(10874416543079064207)
XLA Ops:
  0.0 0.7 %convert_element_type.29 = bf16[16,1,4]{0,2,1:T(4,128)(2,1)S(1)} convert(s32[16,1,4]{0,2,1:T(4,128)} %param.7) | non-fusion elementwise | flops 64 | bytes 384 | tf_op jit(solution)/shard_map/convert_element_type | solution.py:108
  0.7 0.1 copy.10
  0.8 0.1 convert_element_type.30
  0.9 0.7 %broadcast_compare_fusion = pred[16,256]{1,0:T(8,128)(4,1)S(1)} fusion(s32[256]{0:T(256)S(1)} %and_select_fusion, s32[16]{0:T(128)} %bitcast.24), kind=kLoop, calls=%fused_computation.7 | loop fusion | flops 4096 | bytes 5184 | tf_op jit(solution)/shard_map/lt | solution.py:105
  1.6 0.0 copy-start.4
  1.6 1.1 %bitcast_select_fusion = bf16[16,64,256]{2,1,0:T(8,128)(2,1)S(1)} fusion(bf16[16,64,1,256]{3,1,2,0:T(8,128)(2,1)} %param.6, pred[16,256]{1,0:T(8,128)(4,1)S(1)} %broadcast_compare_fusion), kind=kLoop, calls=%fused_computation.4 | loop fusion | flops 262144 | bytes 1052672 | tf_op jit(solution)/shard_map/jit(_where)/select_n | solution.py:105
  2.8 0.7 %collective-permute-start.2 = (bf16[17,64,256]{2,1,0:T(8,128)(2,1)S(1)}, bf16[17,64,256]{2,1,0:T(8,128)(2,1)S(1)}, u32[]{:S(2)}, u32[]{:S(2)}) collective-permute-start(bf16[17,64,256]{2,1,0:T(8,128)(2,1)S(1)} %fusion.1), channel_id=1, source_target_pairs={{0,0},{5,1},{2,2},{7,3},{4,4},{1,5},{6,6},{3,7},{10,8},{15,9},{8,1... | collective-permute-start | bytes 1671176 | tf_op jit(solution)/shard_map/ppermute | solution.py:138
  3.5 0.7 %collective-permute-start.1 = (bf16[17,64,256]{2,1,0:T(8,128)(2,1)S(1)}, bf16[17,64,256]{2,1,0:T(8,128)(2,1)S(1)}, u32[]{:S(2)}, u32[]{:S(2)}) collective-permute-start(bf16[17,64,256]{2,1,0:T(8,128)(2,1)S(1)} %fusion.1), channel_id=1, source_target_pairs={{0,0},{17,1},{10,2},{27,3},{20,4},{5,5},{30,6},{15,7},{8,8},{25,9}... | collective-permute-start | bytes 1671176 | tf_op jit(solution)/shard_map/ppermute | solution.py:137
  4.2 9.3 %collective-permute-start.3 = (bf16[17,64,256]{2,1,0:T(8,128)(2,1)S(1)}, bf16[17,64,256]{2,1,0:T(8,128)(2,1)S(1)}, u32[]{:S(2)}, u32[]{:S(2)}) collective-permute-start(bf16[17,64,256]{2,1,0:T(8,128)(2,1)S(1)} %fusion.1), channel_id=1, source_target_pairs={{2,0},{7,1},{0,2},{5,3},{6,4},{3,5},{4,6},{1,7},{8,8},{13,9},{10,1... | collective-permute-start | bytes 1671176 | tf_op jit(solution)/shard_map/ppermute | solution.py:138
  13.5 1.9 %collective-permute-start = (bf16[17,64,256]{2,1,0:T(8,128)(2,1)S(1)}, bf16[17,64,256]{2,1,0:T(8,128)(2,1)S(1)}, u32[]{:S(2)}, u32[]{:S(2)}) collective-permute-start(bf16[17,64,256]{2,1,0:T(8,128)(2,1)S(1)} %fusion.1), channel_id=1, source_target_pairs={{8,0},{25,1},{2,2},{19,3},{28,4},{13,5},{22,6},{7,7},{0,8},{17,9},... | collective-permute-start | bytes 1671176 | tf_op jit(solution)/shard_map/ppermute | solution.py:137
  15.4 0.0 copy-done.4
  15.4 0.1 copy.11
  15.5 0.6 %reshape.122.want = s32[128]{0:T(128)} reshape(s32[16,8]{1,0:T(8,128)S(1)} %copy.11) | data formatting | bytes 1024 | tf_op jit(solution)/shard_map/reshape | solution.py:125
  16.1 0.0 collective-permute-done.2.b_ref
  16.1 0.0 copy-start.2
  16.1 0.5 %fusion.5.b_cols = s32[64]{0:T(128)} fusion(bf16[17,64,256]{2,1,0:T(8,128)(2,1)S(1)} %collective-permute-done.2.b_ref), kind=kLoop, calls=%fused_computation.17 | loop fusion | flops 64 | bytes 384 | tf_op jit(solution)/shard_map/convert_element_type | solution.py:141
  16.7 0.0 collective-permute-done.1.a_ref
  16.7 0.0 copy-start.3
  16.7 0.6 %fusion.6.a_cols = s32[64]{0:T(128)} fusion(bf16[17,64,256]{2,1,0:T(8,128)(2,1)S(1)} %collective-permute-done.1.a_ref), kind=kLoop, calls=%fused_computation.19 | loop fusion | flops 64 | bytes 384 | tf_op jit(solution)/shard_map/convert_element_type | solution.py:140
  17.3 0.0 copy-done.2
  17.3 0.2 copy-done.3
  17.5 6.7 %shard_map.46 = (f32[16,64,256]{2,1,0:T(8,128)}, f32[16,64,256]{2,1,0:T(8,128)}, s32[1]{0:T(128)}) custom-call(s32[64]{0:T(128)} %fusion.6.a_cols, s32[64]{0:T(128)} %fusion.5.b_cols, s32[128]{0:T(128)} %reshape.122.want, bf16[17,64,256]{2,1,0:T(8,128)(2,1)} %copy-done.3, bf16[17,64,256]{2,1,0:T(8,128)(2,1)} %copy-done.2), custom_call_target="tpu_custom_call" | custom-call | flops 268435456 | bytes 3211264 | tf_op jit(solution)/shard_map/pallas_call | solution.py:84
  24.2 7.6 %collective-permute-done.3.b_ref = bf16[17,64,256]{2,1,0:T(8,128)(2,1)S(1)} collective-permute-done((bf16[17,64,256]{2,1,0:T(8,128)(2,1)S(1)}, bf16[17,64,256]{2,1,0:T(8,128)(2,1)S(1)}, u32[]{:S(2)}, u32[]{:S(2)}) %collective-permute-start.3) | collective-permute-done | bytes 557088 | tf_op jit(solution)/shard_map/ppermute | solution.py:138
  31.8 0.0 copy-start
  31.8 1.1 %fusion.4.b_cols = s32[64]{0:T(128)} fusion(bf16[17,64,256]{2,1,0:T(8,128)(2,1)S(1)} %collective-permute-done.3.b_ref, s32[]{:T(128)} %bitcast.5), kind=kLoop, calls=%fused_computation.15 | loop fusion | flops 128 | bytes 388 | tf_op jit(solution)/shard_map/add | solution.py:141
  32.9 0.0 collective-permute-done.a_ref
  32.9 0.0 copy-start.1
  32.9 1.2 %fusion.8.a_cols = s32[64]{0:T(128)} fusion(bf16[17,64,256]{2,1,0:T(8,128)(2,1)S(1)} %collective-permute-done.a_ref, s32[]{:T(128)} %bitcast.5), kind=kLoop, calls=%fused_computation.22 | loop fusion | flops 128 | bytes 388 | tf_op jit(solution)/shard_map/add | solution.py:140
  34.1 0.0 copy-done
  34.1 0.0 copy-done.1
  34.1 7.4 %shard_map.47 = (f32[16,64,256]{2,1,0:T(8,128)}, f32[16,64,256]{2,1,0:T(8,128)}, s32[1]{0:T(128)}) custom-call(s32[64]{0:T(128)} %fusion.8.a_cols, s32[64]{0:T(128)} %fusion.4.b_cols, s32[128]{0:T(128)} %reshape.122.want, bf16[17,64,256]{2,1,0:T(8,128)(2,1)} %copy-done.1, ...), custom_call_target="tpu_custom_call", output_to_operand_aliasing={{0}: (5, {}), {1}: (6, {})} | custom-call | flops 268435456 | bytes 5308416 | tf_op jit(solution)/shard_map/pallas_call | solution.py:84
  41.5 3.6 %collective-permute-start.4 = (f32[16,64,256]{2,1,0:T(8,128)}, f32[16,64,256]{2,1,0:T(8,128)S(1)}, u32[]{:S(2)}, u32[]{:S(2)}) collective-permute-start(f32[16,64,256]{2,1,0:T(8,128)} %get-tuple-element.26), channel_id=1, source_target_pairs={{0,1},{1,0},{2,3},{3,2},{4,5},{5,4},{6,7},{7,6},{8,9},{9,8},{10,11... | collective-permute-start | bytes 3145736 | tf_op jit(solution)/shard_map/ppermute | solution.py:144
  45.1 2.5 %collective-permute-done.4 = f32[16,64,256]{2,1,0:T(8,128)S(1)} collective-permute-done((f32[16,64,256]{2,1,0:T(8,128)}, f32[16,64,256]{2,1,0:T(8,128)S(1)}, u32[]{:S(2)}, u32[]{:S(2)}) %collective-permute-start.4) | collective-permute-done | bytes 1048608 | tf_op jit(solution)/shard_map/ppermute | solution.py:144
  47.6 1.4 %add_bitcast_fusion = f32[16,64,1,256]{3,1,0,2:T(8,128)S(1)} fusion(f32[16,64,256]{2,1,0:T(8,128)} %get-tuple-element.25, f32[16,64,256]{2,1,0:T(8,128)S(1)} %collective-permute-done.4), kind=kLoop, calls=%fused_computation.2 | loop fusion | flops 262144 | bytes 3145728 | tf_op jit(solution)/shard_map/add | solution.py:145
  49.0 2.0 %copy.12 = f32[16,64,1,256]{3,2,1,0:T(1,128)} copy(f32[16,64,1,256]{3,1,0,2:T(8,128)S(1)} %add_bitcast_fusion) | data formatting | bytes 2097152 | tf_op jit(solution)/shard_map/add | solution.py:145
  (3 shorter events, 0.1 us)
Async XLA Ops:
  1.6 13.8 %copy-start.4 = (s32[16,1,8]{0,2,1:T(8,128)S(1)}, s32[16,1,8]{0,2,1:T(8,128)}, u32[]{:S(2)}) copy-start(s32[16,1,8]{0,2,1:T(8,128)} %param.9) | copy-start | bytes 1540
  2.8 13.3 %collective-permute-start.2 = (bf16[17,64,256]{2,1,0:T(8,128)(2,1)S(1)}, bf16[17,64,256]{2,1,0:T(8,128)(2,1)S(1)}, u32[]{:S(2)}, u32[]{:S(2)}) collective-permute-start(bf16[17,64,256]{2,1,0:T(8,128)(2,1)S(1)} %fusion.1), channel_id=1, source_target_pairs={{0,0},{5,1},{2,2},{7,3},{4,4},{1,5},{6,6},{3,7},{10,8},{15,9},{8,1... | collective-permute-start | bytes 1671176 | tf_op jit(solution)/shard_map/ppermute | solution.py:138
  3.5 13.2 %collective-permute-start.1 = (bf16[17,64,256]{2,1,0:T(8,128)(2,1)S(1)}, bf16[17,64,256]{2,1,0:T(8,128)(2,1)S(1)}, u32[]{:S(2)}, u32[]{:S(2)}) collective-permute-start(bf16[17,64,256]{2,1,0:T(8,128)(2,1)S(1)} %fusion.1), channel_id=1, source_target_pairs={{0,0},{17,1},{10,2},{27,3},{20,4},{5,5},{30,6},{15,7},{8,8},{25,9}... | collective-permute-start | bytes 1671176 | tf_op jit(solution)/shard_map/ppermute | solution.py:137
  4.2 27.6 %collective-permute-start.3 = (bf16[17,64,256]{2,1,0:T(8,128)(2,1)S(1)}, bf16[17,64,256]{2,1,0:T(8,128)(2,1)S(1)}, u32[]{:S(2)}, u32[]{:S(2)}) collective-permute-start(bf16[17,64,256]{2,1,0:T(8,128)(2,1)S(1)} %fusion.1), channel_id=1, source_target_pairs={{2,0},{7,1},{0,2},{5,3},{6,4},{3,5},{4,6},{1,7},{8,8},{13,9},{10,1... | collective-permute-start | bytes 1671176 | tf_op jit(solution)/shard_map/ppermute | solution.py:138
  13.5 19.4 %collective-permute-start = (bf16[17,64,256]{2,1,0:T(8,128)(2,1)S(1)}, bf16[17,64,256]{2,1,0:T(8,128)(2,1)S(1)}, u32[]{:S(2)}, u32[]{:S(2)}) collective-permute-start(bf16[17,64,256]{2,1,0:T(8,128)(2,1)S(1)} %fusion.1), channel_id=1, source_target_pairs={{8,0},{25,1},{2,2},{19,3},{28,4},{13,5},{22,6},{7,7},{0,8},{17,9},... | collective-permute-start | bytes 1671176 | tf_op jit(solution)/shard_map/ppermute | solution.py:137
  16.1 1.2 %copy-start.2 = (bf16[17,64,256]{2,1,0:T(8,128)(2,1)}, bf16[17,64,256]{2,1,0:T(8,128)(2,1)S(1)}, u32[]{:S(2)}) copy-start(bf16[17,64,256]{2,1,0:T(8,128)(2,1)S(1)} %collective-permute-done.2.b_ref) | copy-start | bytes 1671172
  16.7 0.8 %copy-start.3 = (bf16[17,64,256]{2,1,0:T(8,128)(2,1)}, bf16[17,64,256]{2,1,0:T(8,128)(2,1)S(1)}, u32[]{:S(2)}) copy-start(bf16[17,64,256]{2,1,0:T(8,128)(2,1)S(1)} %collective-permute-done.1.a_ref) | copy-start | bytes 1671172
  31.8 2.4 %copy-start = (bf16[17,64,256]{2,1,0:T(8,128)(2,1)}, bf16[17,64,256]{2,1,0:T(8,128)(2,1)S(1)}, u32[]{:S(2)}) copy-start(bf16[17,64,256]{2,1,0:T(8,128)(2,1)S(1)} %collective-permute-done.3.b_ref) | copy-start | bytes 1671172
  32.9 1.2 %copy-start.1 = (bf16[17,64,256]{2,1,0:T(8,128)(2,1)}, bf16[17,64,256]{2,1,0:T(8,128)(2,1)S(1)}, u32[]{:S(2)}) copy-start(bf16[17,64,256]{2,1,0:T(8,128)(2,1)S(1)} %collective-permute-done.a_ref) | copy-start | bytes 1671172
  41.5 6.1 %collective-permute-start.4 = (f32[16,64,256]{2,1,0:T(8,128)}, f32[16,64,256]{2,1,0:T(8,128)S(1)}, u32[]{:S(2)}, u32[]{:S(2)}) collective-permute-start(f32[16,64,256]{2,1,0:T(8,128)} %get-tuple-element.26), channel_id=1, source_target_pairs={{0,1},{1,0},{2,3},{3,2},{4,5},{5,4},{6,7},{7,6},{8,9},{9,8},{10,11... | collective-permute-start | bytes 3145736 | tf_op jit(solution)/shard_map/ppermute | solution.py:144

commit v4 on v3

--- a/solution.py
+++ b/solution.py
@@ -87,7 +87,7 @@
         out_specs=[vmem, vmem, smem],
         scratch_shapes=[
             pltpu.VMEM((rows, seg // width + 1, 2, width, 2 * width), right.dtype),
-            pltpu.VMEM((4 if rows % 4 == 0 else 1, seg, outs * width), right.dtype),
+            pltpu.VMEM((8 if rows % 8 == 0 else 1, seg, outs * width), right.dtype),
             pltpu.SMEM((rows * rows,), jnp.int32),
         ],
         out_shape=[jax.ShapeDtypeStruct((rows, width, share), jnp.float32)] * 2

time: 51.3 us -> 50.8 us (level)
    pallas_call x2, Pallas kernels: 14 us -> 13.5 us  [one_step(): pl.pallas_call(step_kernel, in_specs=[smem] * 3 + [vmem] * (2 + len(sums)...]
where the time goes in v4:
time: 50.8 us; the launch traced here: 50.5 us
  starting transfers between devices  16 us (31%)
  Pallas kernels  13.5 us (27%)
  waiting for transfers between devices  10.3 us (20%)
  other arithmetic  7.47 us (15%)
  local copies, waits for them, and re-layouts  3.12 us (6%)
    pallas_call x2, Pallas kernels, one_step(): pl.pallas_call(step_kernel, in_specs=[smem] * 3 + [vmem] * (2 + len(sums)...  13.5 us
    ppermute x2, starting transfers between devices, per_device(): right = lax.ppermute(payload, ('row', 'col', 'layer'), right_pairs)  9.99 us
    ppermute x2, waiting for transfers between devices, per_device(): right = lax.ppermute(payload, ('row', 'col', 'layer'), right_pairs)  7.84 us
    ppermute x1, starting transfers between devices, per_device(): got = lax.ppermute(theirs, 'layer', [(0, 1), (1, 0)])  3.35 us
    ppermute x2, starting transfers between devices, per_device(): left = lax.ppermute(payload, ('row', 'col', 'layer'), left_pairs)  2.62 us
    ppermute x1, waiting for transfers between devices, per_device(): got = lax.ppermute(theirs, 'layer', [(0, 1), (1, 0)])  2.5 us
    add x1, local copies, waits for them, and re-layouts, per_device(): return mine[:, :, None, :] + got[:, :, None, :]  2.05 us
    add x1, other arithmetic, per_device(): return mine[:, :, None, :] + got[:, :, None, :]  1.36 us
  transfers between devices with their start and end apart: 5, of which 2 were waited for; matrix products, arithmetic and copies ran while one was open for 6% of the time, Pallas kernels for 13%

profile of v4, /device:TPU:0, one launch (start us, length us, event | category | flops | bytes accessed | tf_op | source)
XLA Modules:
  0.0 50.5 jit_solution(3224722792479251016)
XLA Ops:
  0.0 0.7 %convert_element_type.29 = bf16[16,1,4]{0,2,1:T(4,128)(2,1)S(1)} convert(s32[16,1,4]{0,2,1:T(4,128)} %param.7) | non-fusion elementwise | flops 64 | bytes 384 | tf_op jit(solution)/shard_map/convert_element_type | solution.py:108
  0.7 0.1 copy.10
  0.8 0.1 convert_element_type.30
  0.9 0.7 %broadcast_compare_fusion = pred[16,256]{1,0:T(8,128)(4,1)S(1)} fusion(s32[256]{0:T(256)S(1)} %and_select_fusion, s32[16]{0:T(128)} %bitcast.24), kind=kLoop, calls=%fused_computation.7 | loop fusion | flops 4096 | bytes 5184 | tf_op jit(solution)/shard_map/lt | solution.py:105
  1.6 0.0 copy-start.4
  1.6 1.1 %bitcast_select_fusion = bf16[16,64,256]{2,1,0:T(8,128)(2,1)S(1)} fusion(bf16[16,64,1,256]{3,1,2,0:T(8,128)(2,1)} %param.6, pred[16,256]{1,0:T(8,128)(4,1)S(1)} %broadcast_compare_fusion), kind=kLoop, calls=%fused_computation.4 | loop fusion | flops 262144 | bytes 1052672 | tf_op jit(solution)/shard_map/jit(_where)/select_n | solution.py:105
  2.8 0.7 %collective-permute-start.2 = (bf16[17,64,256]{2,1,0:T(8,128)(2,1)S(1)}, bf16[17,64,256]{2,1,0:T(8,128)(2,1)S(1)}, u32[]{:S(2)}, u32[]{:S(2)}) collective-permute-start(bf16[17,64,256]{2,1,0:T(8,128)(2,1)S(1)} %fusion.1), channel_id=1, source_target_pairs={{0,0},{5,1},{2,2},{7,3},{4,4},{1,5},{6,6},{3,7},{10,8},{15,9},{8,1... | collective-permute-start | bytes 1671176 | tf_op jit(solution)/shard_map/ppermute | solution.py:138
  3.5 0.7 %collective-permute-start.1 = (bf16[17,64,256]{2,1,0:T(8,128)(2,1)S(1)}, bf16[17,64,256]{2,1,0:T(8,128)(2,1)S(1)}, u32[]{:S(2)}, u32[]{:S(2)}) collective-permute-start(bf16[17,64,256]{2,1,0:T(8,128)(2,1)S(1)} %fusion.1), channel_id=1, source_target_pairs={{0,0},{17,1},{10,2},{27,3},{20,4},{5,5},{30,6},{15,7},{8,8},{25,9}... | collective-permute-start | bytes 1671176 | tf_op jit(solution)/shard_map/ppermute | solution.py:137
  4.2 9.3 %collective-permute-start.3 = (bf16[17,64,256]{2,1,0:T(8,128)(2,1)S(1)}, bf16[17,64,256]{2,1,0:T(8,128)(2,1)S(1)}, u32[]{:S(2)}, u32[]{:S(2)}) collective-permute-start(bf16[17,64,256]{2,1,0:T(8,128)(2,1)S(1)} %fusion.1), channel_id=1, source_target_pairs={{2,0},{7,1},{0,2},{5,3},{6,4},{3,5},{4,6},{1,7},{8,8},{13,9},{10,1... | collective-permute-start | bytes 1671176 | tf_op jit(solution)/shard_map/ppermute | solution.py:138
  13.5 1.9 %collective-permute-start = (bf16[17,64,256]{2,1,0:T(8,128)(2,1)S(1)}, bf16[17,64,256]{2,1,0:T(8,128)(2,1)S(1)}, u32[]{:S(2)}, u32[]{:S(2)}) collective-permute-start(bf16[17,64,256]{2,1,0:T(8,128)(2,1)S(1)} %fusion.1), channel_id=1, source_target_pairs={{8,0},{25,1},{2,2},{19,3},{28,4},{13,5},{22,6},{7,7},{0,8},{17,9},... | collective-permute-start | bytes 1671176 | tf_op jit(solution)/shard_map/ppermute | solution.py:137
  15.4 0.0 copy-done.4
  15.4 0.1 copy.11
  15.5 0.6 %reshape.122.want = s32[128]{0:T(128)} reshape(s32[16,8]{1,0:T(8,128)S(1)} %copy.11) | data formatting | bytes 1024 | tf_op jit(solution)/shard_map/reshape | solution.py:125
  16.1 0.0 collective-permute-done.2.b_ref
  16.1 0.0 copy-start.2
  16.1 0.5 %fusion.5.b_cols = s32[64]{0:T(128)} fusion(bf16[17,64,256]{2,1,0:T(8,128)(2,1)S(1)} %collective-permute-done.2.b_ref), kind=kLoop, calls=%fused_computation.17 | loop fusion | flops 64 | bytes 384 | tf_op jit(solution)/shard_map/convert_element_type | solution.py:141
  16.7 0.0 collective-permute-done.1.a_ref
  16.7 0.0 copy-start.3
  16.7 0.6 %fusion.6.a_cols = s32[64]{0:T(128)} fusion(bf16[17,64,256]{2,1,0:T(8,128)(2,1)S(1)} %collective-permute-done.1.a_ref), kind=kLoop, calls=%fused_computation.19 | loop fusion | flops 64 | bytes 384 | tf_op jit(solution)/shard_map/convert_element_type | solution.py:140
  17.3 0.0 copy-done.2
  17.3 0.2 copy-done.3
  17.5 6.4 %shard_map.46 = (f32[16,64,256]{2,1,0:T(8,128)}, f32[16,64,256]{2,1,0:T(8,128)}, s32[1]{0:T(128)}) custom-call(s32[64]{0:T(128)} %fusion.6.a_cols, s32[64]{0:T(128)} %fusion.5.b_cols, s32[128]{0:T(128)} %reshape.122.want, bf16[17,64,256]{2,1,0:T(8,128)(2,1)} %copy-done.3, bf16[17,64,256]{2,1,0:T(8,128)(2,1)} %copy-done.2), custom_call_target="tpu_custom_call" | custom-call | flops 268435456 | bytes 3211264 | tf_op jit(solution)/shard_map/pallas_call | solution.py:84
  23.9 7.8 %collective-permute-done.3.b_ref = bf16[17,64,256]{2,1,0:T(8,128)(2,1)S(1)} collective-permute-done((bf16[17,64,256]{2,1,0:T(8,128)(2,1)S(1)}, bf16[17,64,256]{2,1,0:T(8,128)(2,1)S(1)}, u32[]{:S(2)}, u32[]{:S(2)}) %collective-permute-start.3) | collective-permute-done | bytes 557088 | tf_op jit(solution)/shard_map/ppermute | solution.py:138
  31.8 0.0 copy-start
  31.8 1.1 %fusion.4.b_cols = s32[64]{0:T(128)} fusion(bf16[17,64,256]{2,1,0:T(8,128)(2,1)S(1)} %collective-permute-done.3.b_ref, s32[]{:T(128)} %bitcast.5), kind=kLoop, calls=%fused_computation.15 | loop fusion | flops 128 | bytes 388 | tf_op jit(solution)/shard_map/add | solution.py:141
  32.9 0.0 collective-permute-done.a_ref
  32.9 0.0 copy-start.1
  32.9 1.2 %fusion.8.a_cols = s32[64]{0:T(128)} fusion(bf16[17,64,256]{2,1,0:T(8,128)(2,1)S(1)} %collective-permute-done.a_ref, s32[]{:T(128)} %bitcast.5), kind=kLoop, calls=%fused_computation.22 | loop fusion | flops 128 | bytes 388 | tf_op jit(solution)/shard_map/add | solution.py:140
  34.1 0.0 copy-done
  34.1 0.0 copy-done.1
  34.1 7.1 %shard_map.47 = (f32[16,64,256]{2,1,0:T(8,128)}, f32[16,64,256]{2,1,0:T(8,128)}, s32[1]{0:T(128)}) custom-call(s32[64]{0:T(128)} %fusion.8.a_cols, s32[64]{0:T(128)} %fusion.4.b_cols, s32[128]{0:T(128)} %reshape.122.want, bf16[17,64,256]{2,1,0:T(8,128)(2,1)} %copy-done.1, ...), custom_call_target="tpu_custom_call", output_to_operand_aliasing={{0}: (5, {}), {1}: (6, {})} | custom-call | flops 268435456 | bytes 5308416 | tf_op jit(solution)/shard_map/pallas_call | solution.py:84
  41.2 3.4 %collective-permute-start.4 = (f32[16,64,256]{2,1,0:T(8,128)}, f32[16,64,256]{2,1,0:T(8,128)S(1)}, u32[]{:S(2)}, u32[]{:S(2)}) collective-permute-start(f32[16,64,256]{2,1,0:T(8,128)} %get-tuple-element.26), channel_id=1, source_target_pairs={{0,1},{1,0},{2,3},{3,2},{4,5},{5,4},{6,7},{7,6},{8,9},{9,8},{10,11... | collective-permute-start | bytes 3145736 | tf_op jit(solution)/shard_map/ppermute | solution.py:144
  44.6 2.5 %collective-permute-done.4 = f32[16,64,256]{2,1,0:T(8,128)S(1)} collective-permute-done((f32[16,64,256]{2,1,0:T(8,128)}, f32[16,64,256]{2,1,0:T(8,128)S(1)}, u32[]{:S(2)}, u32[]{:S(2)}) %collective-permute-start.4) | collective-permute-done | bytes 1048608 | tf_op jit(solution)/shard_map/ppermute | solution.py:144
  47.1 1.4 %add_bitcast_fusion = f32[16,64,1,256]{3,1,0,2:T(8,128)S(1)} fusion(f32[16,64,256]{2,1,0:T(8,128)} %get-tuple-element.25, f32[16,64,256]{2,1,0:T(8,128)S(1)} %collective-permute-done.4), kind=kLoop, calls=%fused_computation.2 | loop fusion | flops 262144 | bytes 3145728 | tf_op jit(solution)/shard_map/add | solution.py:145
  48.4 2.0 %copy.12 = f32[16,64,1,256]{3,2,1,0:T(1,128)} copy(f32[16,64,1,256]{3,1,0,2:T(8,128)S(1)} %add_bitcast_fusion) | data formatting | bytes 2097152 | tf_op jit(solution)/shard_map/add | solution.py:145
  (3 shorter events, 0.1 us)
Async XLA Ops:
  1.6 13.8 %copy-start.4 = (s32[16,1,8]{0,2,1:T(8,128)S(1)}, s32[16,1,8]{0,2,1:T(8,128)}, u32[]{:S(2)}) copy-start(s32[16,1,8]{0,2,1:T(8,128)} %param.9) | copy-start | bytes 1540
  2.8 13.3 %collective-permute-start.2 = (bf16[17,64,256]{2,1,0:T(8,128)(2,1)S(1)}, bf16[17,64,256]{2,1,0:T(8,128)(2,1)S(1)}, u32[]{:S(2)}, u32[]{:S(2)}) collective-permute-start(bf16[17,64,256]{2,1,0:T(8,128)(2,1)S(1)} %fusion.1), channel_id=1, source_target_pairs={{0,0},{5,1},{2,2},{7,3},{4,4},{1,5},{6,6},{3,7},{10,8},{15,9},{8,1... | collective-permute-start | bytes 1671176 | tf_op jit(solution)/shard_map/ppermute | solution.py:138
  3.5 13.2 %collective-permute-start.1 = (bf16[17,64,256]{2,1,0:T(8,128)(2,1)S(1)}, bf16[17,64,256]{2,1,0:T(8,128)(2,1)S(1)}, u32[]{:S(2)}, u32[]{:S(2)}) collective-permute-start(bf16[17,64,256]{2,1,0:T(8,128)(2,1)S(1)} %fusion.1), channel_id=1, source_target_pairs={{0,0},{17,1},{10,2},{27,3},{20,4},{5,5},{30,6},{15,7},{8,8},{25,9}... | collective-permute-start | bytes 1671176 | tf_op jit(solution)/shard_map/ppermute | solution.py:137
  4.2 27.6 %collective-permute-start.3 = (bf16[17,64,256]{2,1,0:T(8,128)(2,1)S(1)}, bf16[17,64,256]{2,1,0:T(8,128)(2,1)S(1)}, u32[]{:S(2)}, u32[]{:S(2)}) collective-permute-start(bf16[17,64,256]{2,1,0:T(8,128)(2,1)S(1)} %fusion.1), channel_id=1, source_target_pairs={{2,0},{7,1},{0,2},{5,3},{6,4},{3,5},{4,6},{1,7},{8,8},{13,9},{10,1... | collective-permute-start | bytes 1671176 | tf_op jit(solution)/shard_map/ppermute | solution.py:138
  13.5 19.4 %collective-permute-start = (bf16[17,64,256]{2,1,0:T(8,128)(2,1)S(1)}, bf16[17,64,256]{2,1,0:T(8,128)(2,1)S(1)}, u32[]{:S(2)}, u32[]{:S(2)}) collective-permute-start(bf16[17,64,256]{2,1,0:T(8,128)(2,1)S(1)} %fusion.1), channel_id=1, source_target_pairs={{8,0},{25,1},{2,2},{19,3},{28,4},{13,5},{22,6},{7,7},{0,8},{17,9},... | collective-permute-start | bytes 1671176 | tf_op jit(solution)/shard_map/ppermute | solution.py:137
  16.1 1.2 %copy-start.2 = (bf16[17,64,256]{2,1,0:T(8,128)(2,1)}, bf16[17,64,256]{2,1,0:T(8,128)(2,1)S(1)}, u32[]{:S(2)}) copy-start(bf16[17,64,256]{2,1,0:T(8,128)(2,1)S(1)} %collective-permute-done.2.b_ref) | copy-start | bytes 1671172
  16.7 0.8 %copy-start.3 = (bf16[17,64,256]{2,1,0:T(8,128)(2,1)}, bf16[17,64,256]{2,1,0:T(8,128)(2,1)S(1)}, u32[]{:S(2)}) copy-start(bf16[17,64,256]{2,1,0:T(8,128)(2,1)S(1)} %collective-permute-done.1.a_ref) | copy-start | bytes 1671172
  31.8 2.4 %copy-start = (bf16[17,64,256]{2,1,0:T(8,128)(2,1)}, bf16[17,64,256]{2,1,0:T(8,128)(2,1)S(1)}, u32[]{:S(2)}) copy-start(bf16[17,64,256]{2,1,0:T(8,128)(2,1)S(1)} %collective-permute-done.3.b_ref) | copy-start | bytes 1671172
  32.9 1.2 %copy-start.1 = (bf16[17,64,256]{2,1,0:T(8,128)(2,1)}, bf16[17,64,256]{2,1,0:T(8,128)(2,1)S(1)}, u32[]{:S(2)}) copy-start(bf16[17,64,256]{2,1,0:T(8,128)(2,1)S(1)} %collective-permute-done.a_ref) | copy-start | bytes 1671172
  41.2 5.9 %collective-permute-start.4 = (f32[16,64,256]{2,1,0:T(8,128)}, f32[16,64,256]{2,1,0:T(8,128)S(1)}, u32[]{:S(2)}, u32[]{:S(2)}) collective-permute-start(f32[16,64,256]{2,1,0:T(8,128)} %get-tuple-element.26), channel_id=1, source_target_pairs={{0,1},{1,0},{2,3},{3,2},{4,5},{5,4},{6,7},{7,6},{8,9},{9,8},{10,11... | collective-permute-start | bytes 3145736 | tf_op jit(solution)/shard_map/ppermute | solution.py:144

commit v5 on v4

--- a/solution.py
+++ b/solution.py
@@ -8,14 +8,13 @@
 from jax.sharding import PartitionSpec as P
 
 
-def step_kernel(a_cols, b_cols, want, a_ref, b_ref, *refs):
+def step_kernel(width, a_cols, b_cols, want, a_ref, b_ref, *refs):
     if len(refs) == 8:
         mine_in, theirs_in, mine_ref, theirs_ref, tick, place_ref, sel_ref, slot_of = refs
     else:
         mine_in = theirs_in = None
         mine_ref, theirs_ref, tick, place_ref, sel_ref, slot_of = refs
-    width = a_ref.shape[1]
-    seg = a_ref.shape[2]
+    seg = a_ref.shape[1]
     slots = seg // width
     rows = place_ref.shape[0]
     outs = want.shape[0] // rows
@@ -25,7 +24,7 @@
 
     def fill(k, carry):
         for q in range(slots):
-            grp = b_ref[k, :, (q // 2) * 2 * width:(q // 2 + 1) * 2 * width]
+            grp = b_ref[pl.ds(pl.multiple_of(k * width, width), width), (q // 2) * 2 * width:(q // 2 + 1) * 2 * width]
             swap = pltpu.roll(grp, width, 1)
             for i in range(2):
                 src = grp if i == q % 2 else swap
@@ -50,7 +49,8 @@
                     hit = slot_of[k * rows + want[r * outs + 2 * g + i]]
                     picks.append(place_ref[k, hit, i])
                 sel_ref[p * width:(p + 1) * width, g * 2 * width:(g + 1) * 2 * width] = picks[0] + picks[1]
-        prod = jnp.dot(a_ref[r], sel_ref[...], preferred_element_type=jnp.float32)
+        left_rows = a_ref[pl.ds(pl.multiple_of(r * width, width), width), :]
+        prod = jnp.dot(left_rows, sel_ref[...], preferred_element_type=jnp.float32)
         half = prod.shape[1] // 2
         if mine_in is None:
             mine_ref[r] = prod[:, :half]
@@ -69,8 +69,8 @@
     lax.fori_loop(0, rows // group, some_rows, 0)
 
 
-def one_step(mine, theirs, left, right, a_cols, b_cols, want):
-    rows, width, seg = left.shape[0] - 1, left.shape[1], left.shape[2]
+def one_step(mine, theirs, left, right, a_cols, b_cols, want, width):
+    rows, seg = left.shape[0] // width, left.shape[1]
     outs = want.shape[0] // rows
     share = outs // 2 * width
     sums = [] if mine is None else [mine, theirs]
@@ -82,7 +82,7 @@
         bytes_accessed=2 * (left.size + right.size) + 4 * (2 + len(sums)) * rows * width * share,
     )
     return pl.pallas_call(
-        step_kernel,
+        functools.partial(step_kernel, width),
         in_specs=[smem] * 3 + [vmem] * (2 + len(sums)),
         out_specs=[vmem, vmem, smem],
         scratch_shapes=[
@@ -104,9 +104,10 @@
     slot_of_lane = lax.broadcasted_iota(jnp.int32, (1, 1, lanes), 2) // width
     values = jnp.where(slot_of_lane < x_count[:, :, None], values, jnp.zeros((), values.dtype))
     columns = x_cols[:, 0, :].reshape(-1)
-    extra = jnp.zeros((1, width, lanes), values.dtype)
-    extra = extra.at[0, 0, :columns.shape[0]].set(columns.astype(values.dtype))
-    payload = jnp.concatenate([values, extra], axis=0)
+    pad = 16
+    extra = jnp.zeros((pad, lanes), values.dtype)
+    extra = extra.at[0, :columns.shape[0]].set(columns.astype(values.dtype))
+    payload = jnp.concatenate([values.reshape(row_count * width, lanes), extra], axis=0)
 
     rows_n = lax.axis_size("row")
     cols_n = lax.axis_size("col")
@@ -137,9 +138,9 @@
         left = lax.ppermute(payload, ("row", "col", "layer"), left_pairs)
         right = lax.ppermute(payload, ("row", "col", "layer"), right_pairs)
         n = columns.shape[0]
-        a_cols = left[row_count, 0, :n].astype(jnp.int32) + tick
-        b_cols = right[row_count, 0, :n].astype(jnp.int32) + tick
-        mine, theirs, tick = one_step(mine, theirs, left, right, a_cols, b_cols, want)
+        a_cols = left[row_count * width, :n].astype(jnp.int32) + tick
+        b_cols = right[row_count * width, :n].astype(jnp.int32) + tick
+        mine, theirs, tick = one_step(mine, theirs, left, right, a_cols, b_cols, want, width)
 
     got = lax.ppermute(theirs, "layer", [(0, 1), (1, 0)])
     return mine[:, :, None, :] + got[:, :, None, :]

time: 50.8 us -> 49.9 us (0.982)
  waiting for transfers between devices: 10.3 us -> 9.5 us
    ppermute x2, waiting for transfers between devices: 7.84 us -> 6.99 us  [per_device(): right = lax.ppermute(payload, ('row', 'col', 'layer'), right_pairs)]
where the time goes in v5:
time: 49.9 us; the launch traced here: 49.6 us
  starting transfers between devices  15.9 us (32%)
  Pallas kernels  13.5 us (27%)
  waiting for transfers between devices  9.5 us (19%)
  other arithmetic  7.27 us (15%)
  local copies, waits for them, and re-layouts  3.23 us (6%)
    pallas_call x2, Pallas kernels, one_step(): pl.pallas_call(functools.partial(step_kernel, width), in_specs=[smem] * 3...  13.5 us
    ppermute x2, starting transfers between devices, per_device(): right = lax.ppermute(payload, ('row', 'col', 'layer'), right_pairs)  9.99 us
    ppermute x2, waiting for transfers between devices, per_device(): right = lax.ppermute(payload, ('row', 'col', 'layer'), right_pairs)  6.99 us
    ppermute x1, starting transfers between devices, per_device(): got = lax.ppermute(theirs, 'layer', [(0, 1), (1, 0)])  3.34 us
    ppermute x2, starting transfers between devices, per_device(): left = lax.ppermute(payload, ('row', 'col', 'layer'), left_pairs)  2.62 us
    ppermute x1, waiting for transfers between devices, per_device(): got = lax.ppermute(theirs, 'layer', [(0, 1), (1, 0)])  2.5 us
    add x1, local copies, waits for them, and re-layouts, per_device(): return mine[:, :, None, :] + got[:, :, None, :]  2.05 us
    add x1, other arithmetic, per_device(): return mine[:, :, None, :] + got[:, :, None, :]  1.36 us
  transfers between devices with their start and end apart: 5, of which 2 were waited for; matrix products, arithmetic and copies ran while one was open for 6% of the time, Pallas kernels for 13%

profile of v5, /device:TPU:0, one launch (start us, length us, event | category | flops | bytes accessed | tf_op | source)
XLA Modules:
  0.0 49.6 jit_solution(18440575795520335288)
XLA Ops:
  0.0 0.7 %convert_element_type.29 = bf16[16,1,4]{0,2,1:T(4,128)(2,1)S(1)} convert(s32[16,1,4]{0,2,1:T(4,128)} %param.7) | non-fusion elementwise | flops 64 | bytes 384 | tf_op jit(solution)/shard_map/convert_element_type | solution.py:109
  0.7 0.1 copy.10
  0.8 0.1 convert_element_type.30
  0.9 0.7 %broadcast_compare_fusion = pred[16,256]{1,0:T(8,128)(4,1)S(1)} fusion(s32[256]{0:T(256)S(1)} %and_select_fusion, s32[16]{0:T(128)} %bitcast.26), kind=kLoop, calls=%fused_computation.7 | loop fusion | flops 4096 | bytes 5184 | tf_op jit(solution)/shard_map/lt | solution.py:105
  1.6 0.0 copy-start.4
  1.6 1.1 %bitcast_select_fusion = bf16[1024,256]{1,0:T(8,128)(2,1)S(1)} fusion(bf16[16,64,1,256]{3,1,2,0:T(8,128)(2,1)} %param.6, pred[16,256]{1,0:T(8,128)(4,1)S(1)} %broadcast_compare_fusion), kind=kLoop, calls=%fused_computation.3 | loop fusion | flops 262144 | bytes 1052672 | tf_op jit(solution)/shard_map/jit(_where)/select_n | solution.py:105
  2.8 0.7 %collective-permute-start.2 = (bf16[1040,256]{1,0:T(8,128)(2,1)S(1)}, bf16[1040,256]{1,0:T(8,128)(2,1)S(1)}, u32[]{:S(2)}, u32[]{:S(2)}) collective-permute-start(bf16[1040,256]{1,0:T(8,128)(2,1)S(1)} %fusion.1), channel_id=1, source_target_pairs={{0,0},{5,1},{2,2},{7,3},{4,4},{1,5},{6,6},{3,7},{10,8},{15,9},{8,1... | collective-permute-start | bytes 1597448 | tf_op jit(solution)/shard_map/ppermute | solution.py:139
  3.5 0.7 %collective-permute-start.1 = (bf16[1040,256]{1,0:T(8,128)(2,1)S(1)}, bf16[1040,256]{1,0:T(8,128)(2,1)S(1)}, u32[]{:S(2)}, u32[]{:S(2)}) collective-permute-start(bf16[1040,256]{1,0:T(8,128)(2,1)S(1)} %fusion.1), channel_id=1, source_target_pairs={{0,0},{17,1},{10,2},{27,3},{20,4},{5,5},{30,6},{15,7},{8,8},{25,9}... | collective-permute-start | bytes 1597448 | tf_op jit(solution)/shard_map/ppermute | solution.py:138
  4.2 9.3 %collective-permute-start.3 = (bf16[1040,256]{1,0:T(8,128)(2,1)S(1)}, bf16[1040,256]{1,0:T(8,128)(2,1)S(1)}, u32[]{:S(2)}, u32[]{:S(2)}) collective-permute-start(bf16[1040,256]{1,0:T(8,128)(2,1)S(1)} %fusion.1), channel_id=1, source_target_pairs={{2,0},{7,1},{0,2},{5,3},{6,4},{3,5},{4,6},{1,7},{8,8},{13,9},{10,1... | collective-permute-start | bytes 1597448 | tf_op jit(solution)/shard_map/ppermute | solution.py:139
  13.5 1.9 %collective-permute-start = (bf16[1040,256]{1,0:T(8,128)(2,1)S(1)}, bf16[1040,256]{1,0:T(8,128)(2,1)S(1)}, u32[]{:S(2)}, u32[]{:S(2)}) collective-permute-start(bf16[1040,256]{1,0:T(8,128)(2,1)S(1)} %fusion.1), channel_id=1, source_target_pairs={{8,0},{25,1},{2,2},{19,3},{28,4},{13,5},{22,6},{7,7},{0,8},{17,9},... | collective-permute-start | bytes 1597448 | tf_op jit(solution)/shard_map/ppermute | solution.py:138
  15.4 0.0 copy-done.4
  15.4 0.1 copy.11
  15.5 0.6 %reshape.121.want = s32[128]{0:T(128)} reshape(s32[16,8]{1,0:T(8,128)S(1)} %copy.11) | data formatting | bytes 1024 | tf_op jit(solution)/shard_map/reshape | solution.py:126
  16.1 0.0 collective-permute-done.2.b_ref
  16.2 0.0 copy-start.2
  16.2 0.6 %fusion.5.b_cols = s32[64]{0:T(128)} fusion(bf16[1040,256]{1,0:T(8,128)(2,1)S(1)} %collective-permute-done.2.b_ref), kind=kLoop, calls=%fused_computation.17 | loop fusion | flops 64 | bytes 384 | tf_op jit(solution)/shard_map/convert_element_type | solution.py:142
  16.7 0.0 collective-permute-done.1.a_ref
  16.7 0.0 copy-start.3
  16.7 0.5 %fusion.6.a_cols = s32[64]{0:T(128)} fusion(bf16[1040,256]{1,0:T(8,128)(2,1)S(1)} %collective-permute-done.1.a_ref), kind=kLoop, calls=%fused_computation.19 | loop fusion | flops 64 | bytes 384 | tf_op jit(solution)/shard_map/convert_element_type | solution.py:141
  17.3 0.0 copy-done.2
  17.3 0.3 copy-done.3
  17.5 6.4 %shard_map.46 = (f32[16,64,256]{2,1,0:T(8,128)}, f32[16,64,256]{2,1,0:T(8,128)}, s32[1]{0:T(128)}) custom-call(s32[64]{0:T(128)} %fusion.6.a_cols, s32[64]{0:T(128)} %fusion.5.b_cols, s32[128]{0:T(128)} %reshape.121.want, bf16[1040,256]{1,0:T(8,128)(2,1)} %copy-done.3, bf16[1040,256]{1,0:T(8,128)(2,1)} %copy-done.2), custom_call_target="tpu_custom_call" | custom-call | flops 268435456 | bytes 3162112 | tf_op jit(solution)/shard_map/pallas_call | solution.py:84
  24.0 7.0 %collective-permute-done.3.b_ref = bf16[1040,256]{1,0:T(8,128)(2,1)S(1)} collective-permute-done((bf16[1040,256]{1,0:T(8,128)(2,1)S(1)}, bf16[1040,256]{1,0:T(8,128)(2,1)S(1)}, u32[]{:S(2)}, u32[]{:S(2)}) %collective-permute-start.3) | collective-permute-done | bytes 532512 | tf_op jit(solution)/shard_map/ppermute | solution.py:139
  31.0 0.0 copy-start
  31.0 1.1 %fusion.4.b_cols = s32[64]{0:T(128)} fusion(bf16[1040,256]{1,0:T(8,128)(2,1)S(1)} %collective-permute-done.3.b_ref, s32[]{:T(128)} %bitcast.6), kind=kLoop, calls=%fused_computation.15 | loop fusion | flops 128 | bytes 388 | tf_op jit(solution)/shard_map/add | solution.py:142
  32.1 0.0 collective-permute-done.a_ref
  32.1 0.0 copy-start.1
  32.1 1.1 %fusion.8.a_cols = s32[64]{0:T(128)} fusion(bf16[1040,256]{1,0:T(8,128)(2,1)S(1)} %collective-permute-done.a_ref, s32[]{:T(128)} %bitcast.6), kind=kLoop, calls=%fused_computation.22 | loop fusion | flops 128 | bytes 388 | tf_op jit(solution)/shard_map/add | solution.py:141
  33.2 0.0 copy-done
  33.2 0.0 copy-done.1
  33.2 7.1 %shard_map.47 = (f32[16,64,256]{2,1,0:T(8,128)}, f32[16,64,256]{2,1,0:T(8,128)}, s32[1]{0:T(128)}) custom-call(s32[64]{0:T(128)} %fusion.8.a_cols, s32[64]{0:T(128)} %fusion.4.b_cols, s32[128]{0:T(128)} %reshape.121.want, bf16[1040,256]{1,0:T(8,128)(2,1)} %copy-done.1, bf16[1040,256]{1,0:T(8,128)(2,1)} %copy-done, ...), custom_call_target="tpu_custom_call", output_to_operand_aliasing={{0}: (5, {}), {1}: (6, {})} | custom-call | flops 268435456 | bytes 5259264 | tf_op jit(solution)/shard_map/pallas_call | solution.py:84
  40.3 3.3 %collective-permute-start.4 = (f32[16,64,256]{2,1,0:T(8,128)}, f32[16,64,256]{2,1,0:T(8,128)S(1)}, u32[]{:S(2)}, u32[]{:S(2)}) collective-permute-start(f32[16,64,256]{2,1,0:T(8,128)} %get-tuple-element.26), channel_id=1, source_target_pairs={{0,1},{1,0},{2,3},{3,2},{4,5},{5,4},{6,7},{7,6},{8,9},{9,8},{10,11... | collective-permute-start | bytes 3145736 | tf_op jit(solution)/shard_map/ppermute | solution.py:145
  43.7 2.5 %collective-permute-done.4 = f32[16,64,256]{2,1,0:T(8,128)S(1)} collective-permute-done((f32[16,64,256]{2,1,0:T(8,128)}, f32[16,64,256]{2,1,0:T(8,128)S(1)}, u32[]{:S(2)}, u32[]{:S(2)}) %collective-permute-start.4) | collective-permute-done | bytes 1048608 | tf_op jit(solution)/shard_map/ppermute | solution.py:145
  46.2 1.4 %add_bitcast_fusion = f32[16,64,1,256]{3,1,0,2:T(8,128)S(1)} fusion(f32[16,64,256]{2,1,0:T(8,128)} %get-tuple-element.25, f32[16,64,256]{2,1,0:T(8,128)S(1)} %collective-permute-done.4), kind=kLoop, calls=%fused_computation.2 | loop fusion | flops 262144 | bytes 3145728 | tf_op jit(solution)/shard_map/add | solution.py:146
  47.5 2.0 %copy.12 = f32[16,64,1,256]{3,2,1,0:T(1,128)} copy(f32[16,64,1,256]{3,1,0,2:T(8,128)S(1)} %add_bitcast_fusion) | data formatting | bytes 2097152 | tf_op jit(solution)/shard_map/add | solution.py:146
  (3 shorter events, 0.1 us)
Async XLA Ops:
  1.6 13.8 %copy-start.4 = (s32[16,1,8]{0,2,1:T(8,128)S(1)}, s32[16,1,8]{0,2,1:T(8,128)}, u32[]{:S(2)}) copy-start(s32[16,1,8]{0,2,1:T(8,128)} %param.9) | copy-start | bytes 1540
  2.8 13.4 %collective-permute-start.2 = (bf16[1040,256]{1,0:T(8,128)(2,1)S(1)}, bf16[1040,256]{1,0:T(8,128)(2,1)S(1)}, u32[]{:S(2)}, u32[]{:S(2)}) collective-permute-start(bf16[1040,256]{1,0:T(8,128)(2,1)S(1)} %fusion.1), channel_id=1, source_target_pairs={{0,0},{5,1},{2,2},{7,3},{4,4},{1,5},{6,6},{3,7},{10,8},{15,9},{8,1... | collective-permute-start | bytes 1597448 | tf_op jit(solution)/shard_map/ppermute | solution.py:139
  3.5 13.2 %collective-permute-start.1 = (bf16[1040,256]{1,0:T(8,128)(2,1)S(1)}, bf16[1040,256]{1,0:T(8,128)(2,1)S(1)}, u32[]{:S(2)}, u32[]{:S(2)}) collective-permute-start(bf16[1040,256]{1,0:T(8,128)(2,1)S(1)} %fusion.1), channel_id=1, source_target_pairs={{0,0},{17,1},{10,2},{27,3},{20,4},{5,5},{30,6},{15,7},{8,8},{25,9}... | collective-permute-start | bytes 1597448 | tf_op jit(solution)/shard_map/ppermute | solution.py:138
  4.2 26.8 %collective-permute-start.3 = (bf16[1040,256]{1,0:T(8,128)(2,1)S(1)}, bf16[1040,256]{1,0:T(8,128)(2,1)S(1)}, u32[]{:S(2)}, u32[]{:S(2)}) collective-permute-start(bf16[1040,256]{1,0:T(8,128)(2,1)S(1)} %fusion.1), channel_id=1, source_target_pairs={{2,0},{7,1},{0,2},{5,3},{6,4},{3,5},{4,6},{1,7},{8,8},{13,9},{10,1... | collective-permute-start | bytes 1597448 | tf_op jit(solution)/shard_map/ppermute | solution.py:139
  13.5 18.6 %collective-permute-start = (bf16[1040,256]{1,0:T(8,128)(2,1)S(1)}, bf16[1040,256]{1,0:T(8,128)(2,1)S(1)}, u32[]{:S(2)}, u32[]{:S(2)}) collective-permute-start(bf16[1040,256]{1,0:T(8,128)(2,1)S(1)} %fusion.1), channel_id=1, source_target_pairs={{8,0},{25,1},{2,2},{19,3},{28,4},{13,5},{22,6},{7,7},{0,8},{17,9},... | collective-permute-start | bytes 1597448 | tf_op jit(solution)/shard_map/ppermute | solution.py:138
  16.2 1.1 %copy-start.2 = (bf16[1040,256]{1,0:T(8,128)(2,1)}, bf16[1040,256]{1,0:T(8,128)(2,1)S(1)}, u32[]{:S(2)}) copy-start(bf16[1040,256]{1,0:T(8,128)(2,1)S(1)} %collective-permute-done.2.b_ref) | copy-start | bytes 1597444
  16.7 0.8 %copy-start.3 = (bf16[1040,256]{1,0:T(8,128)(2,1)}, bf16[1040,256]{1,0:T(8,128)(2,1)S(1)}, u32[]{:S(2)}) copy-start(bf16[1040,256]{1,0:T(8,128)(2,1)S(1)} %collective-permute-done.1.a_ref) | copy-start | bytes 1597444
  31.0 2.3 %copy-start = (bf16[1040,256]{1,0:T(8,128)(2,1)}, bf16[1040,256]{1,0:T(8,128)(2,1)S(1)}, u32[]{:S(2)}) copy-start(bf16[1040,256]{1,0:T(8,128)(2,1)S(1)} %collective-permute-done.3.b_ref) | copy-start | bytes 1597444
  32.1 1.1 %copy-start.1 = (bf16[1040,256]{1,0:T(8,128)(2,1)}, bf16[1040,256]{1,0:T(8,128)(2,1)S(1)}, u32[]{:S(2)}) copy-start(bf16[1040,256]{1,0:T(8,128)(2,1)S(1)} %collective-permute-done.a_ref) | copy-start | bytes 1597444
  40.3 5.8 %collective-permute-start.4 = (f32[16,64,256]{2,1,0:T(8,128)}, f32[16,64,256]{2,1,0:T(8,128)S(1)}, u32[]{:S(2)}, u32[]{:S(2)}) collective-permute-start(f32[16,64,256]{2,1,0:T(8,128)} %get-tuple-element.26), channel_id=1, source_target_pairs={{0,1},{1,0},{2,3},{3,2},{4,5},{5,4},{6,7},{7,6},{8,9},{9,8},{10,11... | collective-permute-start | bytes 3145736 | tf_op jit(solution)/shard_map/ppermute | solution.py:145

commit v6 on v5

--- a/solution.py
+++ b/solution.py
@@ -34,7 +34,7 @@
             place_ref[k, slots, i] = zero
         return carry
 
-    lax.fori_loop(0, rows, fill, 0)
+    lax.fori_loop(0, rows, fill, 0, unroll=True)
     for n in range(rows * rows):
         slot_of[n] = jnp.int32(slots)
     for n in range(rows * slots):

time: 49.9 us -> 47.7 us (0.956)
  Pallas kernels: 13.5 us -> 11.3 us
  waiting for transfers between devices: 9.5 us -> 10.6 us
  starting transfers between devices: 15.9 us -> 14.9 us
    pallas_call x2, Pallas kernels: 13.5 us -> 11.3 us  [one_step(): pl.pallas_call(functools.partial(step_kernel, width), in_specs=[smem] * 3...]
    ppermute x2, waiting for transfers between devices: 6.99 us -> 8.09 us  [per_device(): right = lax.ppermute(payload, ('row', 'col', 'layer'), right_pairs)]
    ppermute x1, starting transfers between devices: 3.34 us -> 2.24 us  [per_device(): got = lax.ppermute(theirs, 'layer', [(0, 1), (1, 0)])]
  transfers between devices with their start and end apart: 5 -> 5, of which waited for: 2 -> 2; matrix products, arithmetic and copies ran while one was open for 6% -> 6% of each run, Pallas kernels for 13% -> 11%
where the time goes in v6:
time: 47.7 us; the launch traced here: 47.4 us
  starting transfers between devices  14.9 us (31%)
  Pallas kernels  11.3 us (24%)
  waiting for transfers between devices  10.6 us (22%)
  other arithmetic  7.27 us (15%)
  local copies, waits for them, and re-layouts  3.23 us (7%)
    pallas_call x2, Pallas kernels, one_step(): pl.pallas_call(functools.partial(step_kernel, width), in_specs=[smem] * 3...  11.3 us
    ppermute x2, starting transfers between devices, per_device(): right = lax.ppermute(payload, ('row', 'col', 'layer'), right_pairs)  9.99 us
    ppermute x2, waiting for transfers between devices, per_device(): right = lax.ppermute(payload, ('row', 'col', 'layer'), right_pairs)  8.09 us
    ppermute x2, starting transfers between devices, per_device(): left = lax.ppermute(payload, ('row', 'col', 'layer'), left_pairs)  2.62 us
    ppermute x1, waiting for transfers between devices, per_device(): got = lax.ppermute(theirs, 'layer', [(0, 1), (1, 0)])  2.5 us
    ppermute x1, starting transfers between devices, per_device(): got = lax.ppermute(theirs, 'layer', [(0, 1), (1, 0)])  2.24 us
    add x1, local copies, waits for them, and re-layouts, per_device(): return mine[:, :, None, :] + got[:, :, None, :]  2.05 us
    add x1, other arithmetic, per_device(): return mine[:, :, None, :] + got[:, :, None, :]  1.36 us
  transfers between devices with their start and end apart: 5, of which 2 were waited for; matrix products, arithmetic and copies ran while one was open for 6% of the time, Pallas kernels for 11%

profile of v6, /device:TPU:0, one launch (start us, length us, event | category | flops | bytes accessed | tf_op | source)
XLA Modules:
  0.0 47.4 jit_solution(3324773350988279150)
XLA Ops:
  0.0 0.7 %convert_element_type.29 = bf16[16,1,4]{0,2,1:T(4,128)(2,1)S(1)} convert(s32[16,1,4]{0,2,1:T(4,128)} %param.7) | non-fusion elementwise | flops 64 | bytes 384 | tf_op jit(solution)/shard_map/convert_element_type | solution.py:109
  0.7 0.1 copy.10
  0.8 0.1 convert_element_type.30
  0.9 0.7 %broadcast_compare_fusion = pred[16,256]{1,0:T(8,128)(4,1)S(1)} fusion(s32[256]{0:T(256)S(1)} %and_select_fusion, s32[16]{0:T(128)} %bitcast.26), kind=kLoop, calls=%fused_computation.7 | loop fusion | flops 4096 | bytes 5184 | tf_op jit(solution)/shard_map/lt | solution.py:105
  1.6 0.0 copy-start.4
  1.6 1.1 %bitcast_select_fusion = bf16[1024,256]{1,0:T(8,128)(2,1)S(1)} fusion(bf16[16,64,1,256]{3,1,2,0:T(8,128)(2,1)} %param.6, pred[16,256]{1,0:T(8,128)(4,1)S(1)} %broadcast_compare_fusion), kind=kLoop, calls=%fused_computation.3 | loop fusion | flops 262144 | bytes 1052672 | tf_op jit(solution)/shard_map/jit(_where)/select_n | solution.py:105
  2.8 0.7 %collective-permute-start.2 = (bf16[1040,256]{1,0:T(8,128)(2,1)S(1)}, bf16[1040,256]{1,0:T(8,128)(2,1)S(1)}, u32[]{:S(2)}, u32[]{:S(2)}) collective-permute-start(bf16[1040,256]{1,0:T(8,128)(2,1)S(1)} %fusion.1), channel_id=1, source_target_pairs={{0,0},{5,1},{2,2},{7,3},{4,4},{1,5},{6,6},{3,7},{10,8},{15,9},{8,1... | collective-permute-start | bytes 1597448 | tf_op jit(solution)/shard_map/ppermute | solution.py:139
  3.5 0.7 %collective-permute-start.1 = (bf16[1040,256]{1,0:T(8,128)(2,1)S(1)}, bf16[1040,256]{1,0:T(8,128)(2,1)S(1)}, u32[]{:S(2)}, u32[]{:S(2)}) collective-permute-start(bf16[1040,256]{1,0:T(8,128)(2,1)S(1)} %fusion.1), channel_id=1, source_target_pairs={{0,0},{17,1},{10,2},{27,3},{20,4},{5,5},{30,6},{15,7},{8,8},{25,9}... | collective-permute-start | bytes 1597448 | tf_op jit(solution)/shard_map/ppermute | solution.py:138
  4.2 9.3 %collective-permute-start.3 = (bf16[1040,256]{1,0:T(8,128)(2,1)S(1)}, bf16[1040,256]{1,0:T(8,128)(2,1)S(1)}, u32[]{:S(2)}, u32[]{:S(2)}) collective-permute-start(bf16[1040,256]{1,0:T(8,128)(2,1)S(1)} %fusion.1), channel_id=1, source_target_pairs={{2,0},{7,1},{0,2},{5,3},{6,4},{3,5},{4,6},{1,7},{8,8},{13,9},{10,1... | collective-permute-start | bytes 1597448 | tf_op jit(solution)/shard_map/ppermute | solution.py:139
  13.5 1.9 %collective-permute-start = (bf16[1040,256]{1,0:T(8,128)(2,1)S(1)}, bf16[1040,256]{1,0:T(8,128)(2,1)S(1)}, u32[]{:S(2)}, u32[]{:S(2)}) collective-permute-start(bf16[1040,256]{1,0:T(8,128)(2,1)S(1)} %fusion.1), channel_id=1, source_target_pairs={{8,0},{25,1},{2,2},{19,3},{28,4},{13,5},{22,6},{7,7},{0,8},{17,9},... | collective-permute-start | bytes 1597448 | tf_op jit(solution)/shard_map/ppermute | solution.py:138
  15.4 0.0 copy-done.4
  15.4 0.1 copy.11
  15.5 0.6 %reshape.121.want = s32[128]{0:T(128)} reshape(s32[16,8]{1,0:T(8,128)S(1)} %copy.11) | data formatting | bytes 1024 | tf_op jit(solution)/shard_map/reshape | solution.py:126
  16.1 0.0 collective-permute-done.2.b_ref
  16.2 0.0 copy-start.2
  16.2 0.6 %fusion.5.b_cols = s32[64]{0:T(128)} fusion(bf16[1040,256]{1,0:T(8,128)(2,1)S(1)} %collective-permute-done.2.b_ref), kind=kLoop, calls=%fused_computation.17 | loop fusion | flops 64 | bytes 384 | tf_op jit(solution)/shard_map/convert_element_type | solution.py:142
  16.7 0.0 collective-permute-done.1.a_ref
  16.7 0.0 copy-start.3
  16.7 0.5 %fusion.6.a_cols = s32[64]{0:T(128)} fusion(bf16[1040,256]{1,0:T(8,128)(2,1)S(1)} %collective-permute-done.1.a_ref), kind=kLoop, calls=%fused_computation.19 | loop fusion | flops 64 | bytes 384 | tf_op jit(solution)/shard_map/convert_element_type | solution.py:141
  17.3 0.0 copy-done.2
  17.3 0.3 copy-done.3
  17.5 5.3 %shard_map.46 = (f32[16,64,256]{2,1,0:T(8,128)}, f32[16,64,256]{2,1,0:T(8,128)}, s32[1]{0:T(128)}) custom-call(s32[64]{0:T(128)} %fusion.6.a_cols, s32[64]{0:T(128)} %fusion.5.b_cols, s32[128]{0:T(128)} %reshape.121.want, bf16[1040,256]{1,0:T(8,128)(2,1)} %copy-done.3, bf16[1040,256]{1,0:T(8,128)(2,1)} %copy-done.2), custom_call_target="tpu_custom_call" | custom-call | flops 268435456 | bytes 3162112 | tf_op jit(solution)/shard_map/pallas_call | solution.py:84
  22.9 8.1 %collective-permute-done.3.b_ref = bf16[1040,256]{1,0:T(8,128)(2,1)S(1)} collective-permute-done((bf16[1040,256]{1,0:T(8,128)(2,1)S(1)}, bf16[1040,256]{1,0:T(8,128)(2,1)S(1)}, u32[]{:S(2)}, u32[]{:S(2)}) %collective-permute-start.3) | collective-permute-done | bytes 532512 | tf_op jit(solution)/shard_map/ppermute | solution.py:139
  31.0 0.0 copy-start
  31.0 1.1 %fusion.4.b_cols = s32[64]{0:T(128)} fusion(bf16[1040,256]{1,0:T(8,128)(2,1)S(1)} %collective-permute-done.3.b_ref, s32[]{:T(128)} %bitcast.6), kind=kLoop, calls=%fused_computation.15 | loop fusion | flops 128 | bytes 388 | tf_op jit(solution)/shard_map/add | solution.py:142
  32.1 0.0 collective-permute-done.a_ref
  32.1 0.0 copy-start.1
  32.1 1.1 %fusion.8.a_cols = s32[64]{0:T(128)} fusion(bf16[1040,256]{1,0:T(8,128)(2,1)S(1)} %collective-permute-done.a_ref, s32[]{:T(128)} %bitcast.6), kind=kLoop, calls=%fused_computation.22 | loop fusion | flops 128 | bytes 388 | tf_op jit(solution)/shard_map/add | solution.py:141
  33.2 0.0 copy-done
  33.2 0.0 copy-done.1
  33.2 6.0 %shard_map.47 = (f32[16,64,256]{2,1,0:T(8,128)}, f32[16,64,256]{2,1,0:T(8,128)}, s32[1]{0:T(128)}) custom-call(s32[64]{0:T(128)} %fusion.8.a_cols, s32[64]{0:T(128)} %fusion.4.b_cols, s32[128]{0:T(128)} %reshape.121.want, bf16[1040,256]{1,0:T(8,128)(2,1)} %copy-done.1, bf16[1040,256]{1,0:T(8,128)(2,1)} %copy-done, ...), custom_call_target="tpu_custom_call", output_to_operand_aliasing={{0}: (5, {}), {1}: (6, {})} | custom-call | flops 268435456 | bytes 5259264 | tf_op jit(solution)/shard_map/pallas_call | solution.py:84
  39.2 2.2 %collective-permute-start.4 = (f32[16,64,256]{2,1,0:T(8,128)}, f32[16,64,256]{2,1,0:T(8,128)S(1)}, u32[]{:S(2)}, u32[]{:S(2)}) collective-permute-start(f32[16,64,256]{2,1,0:T(8,128)} %get-tuple-element.26), channel_id=1, source_target_pairs={{0,1},{1,0},{2,3},{3,2},{4,5},{5,4},{6,7},{7,6},{8,9},{9,8},{10,11... | collective-permute-start | bytes 3145736 | tf_op jit(solution)/shard_map/ppermute | solution.py:145
  41.5 2.5 %collective-permute-done.4 = f32[16,64,256]{2,1,0:T(8,128)S(1)} collective-permute-done((f32[16,64,256]{2,1,0:T(8,128)}, f32[16,64,256]{2,1,0:T(8,128)S(1)}, u32[]{:S(2)}, u32[]{:S(2)}) %collective-permute-start.4) | collective-permute-done | bytes 1048608 | tf_op jit(solution)/shard_map/ppermute | solution.py:145
  44.0 1.4 %add_bitcast_fusion = f32[16,64,1,256]{3,1,0,2:T(8,128)S(1)} fusion(f32[16,64,256]{2,1,0:T(8,128)} %get-tuple-element.25, f32[16,64,256]{2,1,0:T(8,128)S(1)} %collective-permute-done.4), kind=kLoop, calls=%fused_computation.2 | loop fusion | flops 262144 | bytes 3145728 | tf_op jit(solution)/shard_map/add | solution.py:146
  45.3 2.0 %copy.12 = f32[16,64,1,256]{3,2,1,0:T(1,128)} copy(f32[16,64,1,256]{3,1,0,2:T(8,128)S(1)} %add_bitcast_fusion) | data formatting | bytes 2097152 | tf_op jit(solution)/shard_map/add | solution.py:146
  (3 shorter events, 0.1 us)
Async XLA Ops:
  1.6 13.8 %copy-start.4 = (s32[16,1,8]{0,2,1:T(8,128)S(1)}, s32[16,1,8]{0,2,1:T(8,128)}, u32[]{:S(2)}) copy-start(s32[16,1,8]{0,2,1:T(8,128)} %param.9) | copy-start | bytes 1540
  2.8 13.4 %collective-permute-start.2 = (bf16[1040,256]{1,0:T(8,128)(2,1)S(1)}, bf16[1040,256]{1,0:T(8,128)(2,1)S(1)}, u32[]{:S(2)}, u32[]{:S(2)}) collective-permute-start(bf16[1040,256]{1,0:T(8,128)(2,1)S(1)} %fusion.1), channel_id=1, source_target_pairs={{0,0},{5,1},{2,2},{7,3},{4,4},{1,5},{6,6},{3,7},{10,8},{15,9},{8,1... | collective-permute-start | bytes 1597448 | tf_op jit(solution)/shard_map/ppermute | solution.py:139
  3.5 13.2 %collective-permute-start.1 = (bf16[1040,256]{1,0:T(8,128)(2,1)S(1)}, bf16[1040,256]{1,0:T(8,128)(2,1)S(1)}, u32[]{:S(2)}, u32[]{:S(2)}) collective-permute-start(bf16[1040,256]{1,0:T(8,128)(2,1)S(1)} %fusion.1), channel_id=1, source_target_pairs={{0,0},{17,1},{10,2},{27,3},{20,4},{5,5},{30,6},{15,7},{8,8},{25,9}... | collective-permute-start | bytes 1597448 | tf_op jit(solution)/shard_map/ppermute | solution.py:138
  4.2 26.8 %collective-permute-start.3 = (bf16[1040,256]{1,0:T(8,128)(2,1)S(1)}, bf16[1040,256]{1,0:T(8,128)(2,1)S(1)}, u32[]{:S(2)}, u32[]{:S(2)}) collective-permute-start(bf16[1040,256]{1,0:T(8,128)(2,1)S(1)} %fusion.1), channel_id=1, source_target_pairs={{2,0},{7,1},{0,2},{5,3},{6,4},{3,5},{4,6},{1,7},{8,8},{13,9},{10,1... | collective-permute-start | bytes 1597448 | tf_op jit(solution)/shard_map/ppermute | solution.py:139
  13.5 18.6 %collective-permute-start = (bf16[1040,256]{1,0:T(8,128)(2,1)S(1)}, bf16[1040,256]{1,0:T(8,128)(2,1)S(1)}, u32[]{:S(2)}, u32[]{:S(2)}) collective-permute-start(bf16[1040,256]{1,0:T(8,128)(2,1)S(1)} %fusion.1), channel_id=1, source_target_pairs={{8,0},{25,1},{2,2},{19,3},{28,4},{13,5},{22,6},{7,7},{0,8},{17,9},... | collective-permute-start | bytes 1597448 | tf_op jit(solution)/shard_map/ppermute | solution.py:138
  16.2 1.1 %copy-start.2 = (bf16[1040,256]{1,0:T(8,128)(2,1)}, bf16[1040,256]{1,0:T(8,128)(2,1)S(1)}, u32[]{:S(2)}) copy-start(bf16[1040,256]{1,0:T(8,128)(2,1)S(1)} %collective-permute-done.2.b_ref) | copy-start | bytes 1597444
  16.7 0.8 %copy-start.3 = (bf16[1040,256]{1,0:T(8,128)(2,1)}, bf16[1040,256]{1,0:T(8,128)(2,1)S(1)}, u32[]{:S(2)}) copy-start(bf16[1040,256]{1,0:T(8,128)(2,1)S(1)} %collective-permute-done.1.a_ref) | copy-start | bytes 1597444
  31.0 2.3 %copy-start = (bf16[1040,256]{1,0:T(8,128)(2,1)}, bf16[1040,256]{1,0:T(8,128)(2,1)S(1)}, u32[]{:S(2)}) copy-start(bf16[1040,256]{1,0:T(8,128)(2,1)S(1)} %collective-permute-done.3.b_ref) | copy-start | bytes 1597444
  32.1 1.1 %copy-start.1 = (bf16[1040,256]{1,0:T(8,128)(2,1)}, bf16[1040,256]{1,0:T(8,128)(2,1)S(1)}, u32[]{:S(2)}) copy-start(bf16[1040,256]{1,0:T(8,128)(2,1)S(1)} %collective-permute-done.a_ref) | copy-start | bytes 1597444
  39.2 4.7 %collective-permute-start.4 = (f32[16,64,256]{2,1,0:T(8,128)}, f32[16,64,256]{2,1,0:T(8,128)S(1)}, u32[]{:S(2)}, u32[]{:S(2)}) collective-permute-start(f32[16,64,256]{2,1,0:T(8,128)} %get-tuple-element.26), channel_id=1, source_target_pairs={{0,1},{1,0},{2,3},{3,2},{4,5},{5,4},{6,7},{7,6},{8,9},{9,8},{10,11... | collective-permute-start | bytes 3145736 | tf_op jit(solution)/shard_map/ppermute | solution.py:145

commit v7 on v6

--- a/solution.py
+++ b/solution.py
@@ -66,7 +66,7 @@
             one_row(group * n + m, sel_ref.at[m])
         return carry
 
-    lax.fori_loop(0, rows // group, some_rows, 0)
+    lax.fori_loop(0, rows // group, some_rows, 0, unroll=True)
 
 
 def one_step(mine, theirs, left, right, a_cols, b_cols, want, width):
@@ -87,7 +87,7 @@
         out_specs=[vmem, vmem, smem],
         scratch_shapes=[
             pltpu.VMEM((rows, seg // width + 1, 2, width, 2 * width), right.dtype),
-            pltpu.VMEM((8 if rows % 8 == 0 else 1, seg, outs * width), right.dtype),
+            pltpu.VMEM((16 if rows % 16 == 0 else 1, seg, outs * width), right.dtype),
             pltpu.SMEM((rows * rows,), jnp.int32),
         ],
         out_shape=[jax.ShapeDtypeStruct((rows, width, share), jnp.float32)] * 2
@@ -138,7 +138,7 @@
         left = lax.ppermute(payload, ("row", "col", "layer"), left_pairs)
         right = lax.ppermute(payload, ("row", "col", "layer"), right_pairs)
         n = columns.shape[0]
-        a_cols = left[row_count * width, :n].astype(jnp.int32) + tick
+        a_cols = left[row_count * width, :n].astype(jnp.int32)
         b_cols = right[row_count * width, :n].astype(jnp.int32) + tick
         mine, theirs, tick = one_step(mine, theirs, left, right, a_cols, b_cols, want, width)
 

time: 47.7 us -> 46.7 us (0.979)
  other arithmetic: 7.27 us -> 6.7 us
    ppermute x2, waiting for transfers between devices: 8.09 us -> 0.13 us  [per_device(): right = lax.ppermute(payload, ('row', 'col', 'layer'), right_pairs)]
    ppermute x2, waiting for transfers between devices: 0.01 us -> 7.63 us  [per_device(): left = lax.ppermute(payload, ('row', 'col', 'layer'), left_pairs)]
    add x1 -> x0, other arithmetic: 1.11 us -> none  [per_device(): a_cols = left[row_count * width, :n].astype(jnp.int32) + tick]
    convert_element_type x1 -> x2, other arithmetic: 0.54 us -> 1.09 us  [per_device(): a_cols = left[row_count * width, :n].astype(jnp.int32)]
  transfers between devices with their start and end apart: 5 -> 5, of which waited for: 2 -> 3; matrix products, arithmetic and copies ran while one was open for 6% -> 5% of each run, Pallas kernels for 11% -> 11%
where the time goes in v7:
time: 46.7 us; the launch traced here: 46.4 us
  starting transfers between devices  15.2 us (33%)
  Pallas kernels  11 us (24%)
  waiting for transfers between devices  10.3 us (22%)
  other arithmetic  6.7 us (14%)
  local copies, waits for them, and re-layouts  3.23 us (7%)
    pallas_call x2, Pallas kernels, one_step(): pl.pallas_call(functools.partial(step_kernel, width), in_specs=[smem] * 3...  11 us
    ppermute x2, starting transfers between devices, per_device(): right = lax.ppermute(payload, ('row', 'col', 'layer'), right_pairs)  9.99 us
    ppermute x2, waiting for transfers between devices, per_device(): left = lax.ppermute(payload, ('row', 'col', 'layer'), left_pairs)  7.63 us
    ppermute x2, starting transfers between devices, per_device(): left = lax.ppermute(payload, ('row', 'col', 'layer'), left_pairs)  2.62 us
    ppermute x1, starting transfers between devices, per_device(): got = lax.ppermute(theirs, 'layer', [(0, 1), (1, 0)])  2.57 us
    ppermute x1, waiting for transfers between devices, per_device(): got = lax.ppermute(theirs, 'layer', [(0, 1), (1, 0)])  2.5 us
    add x1, local copies, waits for them, and re-layouts, per_device(): return mine[:, :, None, :] + got[:, :, None, :]  2.05 us
    add x1, other arithmetic, per_device(): return mine[:, :, None, :] + got[:, :, None, :]  1.36 us
  transfers between devices with their start and end apart: 5, of which 3 were waited for; matrix products, arithmetic and copies ran while one was open for 5% of the time, Pallas kernels for 11%

profile of v7, /device:TPU:0, one launch (start us, length us, event | category | flops | bytes accessed | tf_op | source)
XLA Modules:
  0.0 46.4 jit_solution(1411305061346318230)
XLA Ops:
  0.0 0.7 %convert_element_type.30 = bf16[16,1,4]{0,2,1:T(4,128)(2,1)S(1)} convert(s32[16,1,4]{0,2,1:T(4,128)} %param.7) | non-fusion elementwise | flops 64 | bytes 384 | tf_op jit(solution)/shard_map/convert_element_type | solution.py:109
  0.7 0.1 copy.10
  0.8 0.1 convert_element_type.31
  0.9 0.7 %broadcast_compare_fusion = pred[16,256]{1,0:T(8,128)(4,1)S(1)} fusion(s32[256]{0:T(256)S(1)} %and_select_fusion, s32[16]{0:T(128)} %bitcast.29), kind=kLoop, calls=%fused_computation.7 | loop fusion | flops 4096 | bytes 5184 | tf_op jit(solution)/shard_map/lt | solution.py:105
  1.6 0.0 copy-start.4
  1.6 1.1 %bitcast_select_fusion = bf16[1024,256]{1,0:T(8,128)(2,1)S(1)} fusion(bf16[16,64,1,256]{3,1,2,0:T(8,128)(2,1)} %param.6, pred[16,256]{1,0:T(8,128)(4,1)S(1)} %broadcast_compare_fusion), kind=kLoop, calls=%fused_computation.3 | loop fusion | flops 262144 | bytes 1052672 | tf_op jit(solution)/shard_map/jit(_where)/select_n | solution.py:105
  2.8 0.7 %collective-permute-start.3 = (bf16[1040,256]{1,0:T(8,128)(2,1)S(1)}, bf16[1040,256]{1,0:T(8,128)(2,1)S(1)}, u32[]{:S(2)}, u32[]{:S(2)}) collective-permute-start(bf16[1040,256]{1,0:T(8,128)(2,1)S(1)} %fusion.1), channel_id=1, source_target_pairs={{0,0},{5,1},{2,2},{7,3},{4,4},{1,5},{6,6},{3,7},{10,8},{15,9},{8,1... | collective-permute-start | bytes 1597448 | tf_op jit(solution)/shard_map/ppermute | solution.py:139
  3.5 0.7 %collective-permute-start.2 = (bf16[1040,256]{1,0:T(8,128)(2,1)S(1)}, bf16[1040,256]{1,0:T(8,128)(2,1)S(1)}, u32[]{:S(2)}, u32[]{:S(2)}) collective-permute-start(bf16[1040,256]{1,0:T(8,128)(2,1)S(1)} %fusion.1), channel_id=1, source_target_pairs={{0,0},{17,1},{10,2},{27,3},{20,4},{5,5},{30,6},{15,7},{8,8},{25,9}... | collective-permute-start | bytes 1597448 | tf_op jit(solution)/shard_map/ppermute | solution.py:138
  4.2 9.3 %collective-permute-start.1 = (bf16[1040,256]{1,0:T(8,128)(2,1)S(1)}, bf16[1040,256]{1,0:T(8,128)(2,1)S(1)}, u32[]{:S(2)}, u32[]{:S(2)}) collective-permute-start(bf16[1040,256]{1,0:T(8,128)(2,1)S(1)} %fusion.1), channel_id=1, source_target_pairs={{2,0},{7,1},{0,2},{5,3},{6,4},{3,5},{4,6},{1,7},{8,8},{13,9},{10,1... | collective-permute-start | bytes 1597448 | tf_op jit(solution)/shard_map/ppermute | solution.py:139
  13.5 1.9 %collective-permute-start = (bf16[1040,256]{1,0:T(8,128)(2,1)S(1)}, bf16[1040,256]{1,0:T(8,128)(2,1)S(1)}, u32[]{:S(2)}, u32[]{:S(2)}) collective-permute-start(bf16[1040,256]{1,0:T(8,128)(2,1)S(1)} %fusion.1), channel_id=1, source_target_pairs={{8,0},{25,1},{2,2},{19,3},{28,4},{13,5},{22,6},{7,7},{0,8},{17,9},... | collective-permute-start | bytes 1597448 | tf_op jit(solution)/shard_map/ppermute | solution.py:138
  15.4 0.0 copy-done.4
  15.4 0.1 copy.11
  15.5 0.6 %reshape.120.want = s32[128]{0:T(128)} reshape(s32[16,8]{1,0:T(8,128)S(1)} %copy.11) | data formatting | bytes 1024 | tf_op jit(solution)/shard_map/reshape | solution.py:126
  16.1 0.0 collective-permute-done.3.b_ref
  16.2 0.0 copy-start.2
  16.2 0.6 %fusion.3.b_cols = s32[64]{0:T(128)} fusion(bf16[1040,256]{1,0:T(8,128)(2,1)S(1)} %collective-permute-done.3.b_ref), kind=kLoop, calls=%fused_computation.14 | loop fusion | flops 64 | bytes 384 | tf_op jit(solution)/shard_map/convert_element_type | solution.py:142
  16.7 0.0 collective-permute-done.2.a_ref
  16.7 0.0 copy-start.3
  16.7 0.5 %fusion.4.a_cols = s32[64]{0:T(128)} fusion(bf16[1040,256]{1,0:T(8,128)(2,1)S(1)} %collective-permute-done.2.a_ref), kind=kLoop, calls=%fused_computation.16 | loop fusion | flops 64 | bytes 384 | tf_op jit(solution)/shard_map/convert_element_type | solution.py:141
  17.3 0.0 copy-done.2
  17.3 0.3 copy-done.3
  17.5 5.1 %shard_map.46 = (f32[16,64,256]{2,1,0:T(8,128)}, f32[16,64,256]{2,1,0:T(8,128)}, s32[1]{0:T(128)}) custom-call(s32[64]{0:T(128)} %fusion.4.a_cols, s32[64]{0:T(128)} %fusion.3.b_cols, s32[128]{0:T(128)} %reshape.120.want, bf16[1040,256]{1,0:T(8,128)(2,1)} %copy-done.3, bf16[1040,256]{1,0:T(8,128)(2,1)} %copy-done.2), custom_call_target="tpu_custom_call" | custom-call | flops 268435456 | bytes 3162112 | tf_op jit(solution)/shard_map/pallas_call | solution.py:84
  22.7 7.6 %collective-permute-done.a_ref = bf16[1040,256]{1,0:T(8,128)(2,1)S(1)} collective-permute-done((bf16[1040,256]{1,0:T(8,128)(2,1)S(1)}, bf16[1040,256]{1,0:T(8,128)(2,1)S(1)}, u32[]{:S(2)}, u32[]{:S(2)}) %collective-permute-start) | collective-permute-done | bytes 532512 | tf_op jit(solution)/shard_map/ppermute | solution.py:138
  30.3 0.0 copy-start.1
  30.3 0.5 %fusion.7.a_cols = s32[64]{0:T(128)} fusion(bf16[1040,256]{1,0:T(8,128)(2,1)S(1)} %collective-permute-done.a_ref), kind=kLoop, calls=%fused_computation.21 | loop fusion | flops 64 | bytes 384 | tf_op jit(solution)/shard_map/convert_element_type | solution.py:141
  30.8 0.1 collective-permute-done.1.b_ref
  31.0 0.0 copy-start
  31.0 1.1 %fusion.6.b_cols = s32[64]{0:T(128)} fusion(bf16[1040,256]{1,0:T(8,128)(2,1)S(1)} %collective-permute-done.1.b_ref, s32[]{:T(128)} %bitcast.7), kind=kLoop, calls=%fused_computation.19 | loop fusion | flops 128 | bytes 388 | tf_op jit(solution)/shard_map/add | solution.py:142
  32.1 0.0 copy-done.1
  32.1 0.0 copy-done
  32.1 5.8 %shard_map.47 = (f32[16,64,256]{2,1,0:T(8,128)}, f32[16,64,256]{2,1,0:T(8,128)}, s32[1]{0:T(128)}) custom-call(s32[64]{0:T(128)} %fusion.7.a_cols, s32[64]{0:T(128)} %fusion.6.b_cols, s32[128]{0:T(128)} %reshape.120.want, bf16[1040,256]{1,0:T(8,128)(2,1)} %copy-done.1, bf16[1040,256]{1,0:T(8,128)(2,1)} %copy-done, ...), custom_call_target="tpu_custom_call", output_to_operand_aliasing={{0}: (5, {}), {1}: (6, {})} | custom-call | flops 268435456 | bytes 5259264 | tf_op jit(solution)/shard_map/pallas_call | solution.py:84
  37.9 2.6 %collective-permute-start.4 = (f32[16,64,256]{2,1,0:T(8,128)}, f32[16,64,256]{2,1,0:T(8,128)S(1)}, u32[]{:S(2)}, u32[]{:S(2)}) collective-permute-start(f32[16,64,256]{2,1,0:T(8,128)} %get-tuple-element.26), channel_id=1, source_target_pairs={{0,1},{1,0},{2,3},{3,2},{4,5},{5,4},{6,7},{7,6},{8,9},{9,8},{10,11... | collective-permute-start | bytes 3145736 | tf_op jit(solution)/shard_map/ppermute | solution.py:145
  40.5 2.5 %collective-permute-done.4 = f32[16,64,256]{2,1,0:T(8,128)S(1)} collective-permute-done((f32[16,64,256]{2,1,0:T(8,128)}, f32[16,64,256]{2,1,0:T(8,128)S(1)}, u32[]{:S(2)}, u32[]{:S(2)}) %collective-permute-start.4) | collective-permute-done | bytes 1048608 | tf_op jit(solution)/shard_map/ppermute | solution.py:145
  43.0 1.4 %add_bitcast_fusion = f32[16,64,1,256]{3,1,0,2:T(8,128)S(1)} fusion(f32[16,64,256]{2,1,0:T(8,128)} %get-tuple-element.25, f32[16,64,256]{2,1,0:T(8,128)S(1)} %collective-permute-done.4), kind=kLoop, calls=%fused_computation.2 | loop fusion | flops 262144 | bytes 3145728 | tf_op jit(solution)/shard_map/add | solution.py:146
  44.4 2.0 %copy.12 = f32[16,64,1,256]{3,2,1,0:T(1,128)} copy(f32[16,64,1,256]{3,1,0,2:T(8,128)S(1)} %add_bitcast_fusion) | data formatting | bytes 2097152 | tf_op jit(solution)/shard_map/add | solution.py:146
  (3 shorter events, 0.1 us)
Async XLA Ops:
  1.6 13.8 %copy-start.4 = (s32[16,1,8]{0,2,1:T(8,128)S(1)}, s32[16,1,8]{0,2,1:T(8,128)}, u32[]{:S(2)}) copy-start(s32[16,1,8]{0,2,1:T(8,128)} %param.9) | copy-start | bytes 1540
  2.8 13.4 %collective-permute-start.3 = (bf16[1040,256]{1,0:T(8,128)(2,1)S(1)}, bf16[1040,256]{1,0:T(8,128)(2,1)S(1)}, u32[]{:S(2)}, u32[]{:S(2)}) collective-permute-start(bf16[1040,256]{1,0:T(8,128)(2,1)S(1)} %fusion.1), channel_id=1, source_target_pairs={{0,0},{5,1},{2,2},{7,3},{4,4},{1,5},{6,6},{3,7},{10,8},{15,9},{8,1... | collective-permute-start | bytes 1597448 | tf_op jit(solution)/shard_map/ppermute | solution.py:139
  3.5 13.2 %collective-permute-start.2 = (bf16[1040,256]{1,0:T(8,128)(2,1)S(1)}, bf16[1040,256]{1,0:T(8,128)(2,1)S(1)}, u32[]{:S(2)}, u32[]{:S(2)}) collective-permute-start(bf16[1040,256]{1,0:T(8,128)(2,1)S(1)} %fusion.1), channel_id=1, source_target_pairs={{0,0},{17,1},{10,2},{27,3},{20,4},{5,5},{30,6},{15,7},{8,8},{25,9}... | collective-permute-start | bytes 1597448 | tf_op jit(solution)/shard_map/ppermute | solution.py:138
  4.2 26.8 %collective-permute-start.1 = (bf16[1040,256]{1,0:T(8,128)(2,1)S(1)}, bf16[1040,256]{1,0:T(8,128)(2,1)S(1)}, u32[]{:S(2)}, u32[]{:S(2)}) collective-permute-start(bf16[1040,256]{1,0:T(8,128)(2,1)S(1)} %fusion.1), channel_id=1, source_target_pairs={{2,0},{7,1},{0,2},{5,3},{6,4},{3,5},{4,6},{1,7},{8,8},{13,9},{10,1... | collective-permute-start | bytes 1597448 | tf_op jit(solution)/shard_map/ppermute | solution.py:139
  13.5 16.8 %collective-permute-start = (bf16[1040,256]{1,0:T(8,128)(2,1)S(1)}, bf16[1040,256]{1,0:T(8,128)(2,1)S(1)}, u32[]{:S(2)}, u32[]{:S(2)}) collective-permute-start(bf16[1040,256]{1,0:T(8,128)(2,1)S(1)} %fusion.1), channel_id=1, source_target_pairs={{8,0},{25,1},{2,2},{19,3},{28,4},{13,5},{22,6},{7,7},{0,8},{17,9},... | collective-permute-start | bytes 1597448 | tf_op jit(solution)/shard_map/ppermute | solution.py:138
  16.2 1.1 %copy-start.2 = (bf16[1040,256]{1,0:T(8,128)(2,1)}, bf16[1040,256]{1,0:T(8,128)(2,1)S(1)}, u32[]{:S(2)}) copy-start(bf16[1040,256]{1,0:T(8,128)(2,1)S(1)} %collective-permute-done.3.b_ref) | copy-start | bytes 1597444
  16.7 0.8 %copy-start.3 = (bf16[1040,256]{1,0:T(8,128)(2,1)}, bf16[1040,256]{1,0:T(8,128)(2,1)S(1)}, u32[]{:S(2)}) copy-start(bf16[1040,256]{1,0:T(8,128)(2,1)S(1)} %collective-permute-done.2.a_ref) | copy-start | bytes 1597444
  30.3 1.8 %copy-start.1 = (bf16[1040,256]{1,0:T(8,128)(2,1)}, bf16[1040,256]{1,0:T(8,128)(2,1)S(1)}, u32[]{:S(2)}) copy-start(bf16[1040,256]{1,0:T(8,128)(2,1)S(1)} %collective-permute-done.a_ref) | copy-start | bytes 1597444
  31.0 1.1 %copy-start = (bf16[1040,256]{1,0:T(8,128)(2,1)}, bf16[1040,256]{1,0:T(8,128)(2,1)S(1)}, u32[]{:S(2)}) copy-start(bf16[1040,256]{1,0:T(8,128)(2,1)S(1)} %collective-permute-done.1.b_ref) | copy-start | bytes 1597444
  37.9 5.1 %collective-permute-start.4 = (f32[16,64,256]{2,1,0:T(8,128)}, f32[16,64,256]{2,1,0:T(8,128)S(1)}, u32[]{:S(2)}, u32[]{:S(2)}) collective-permute-start(f32[16,64,256]{2,1,0:T(8,128)} %get-tuple-element.26), channel_id=1, source_target_pairs={{0,1},{1,0},{2,3},{3,2},{4,5},{5,4},{6,7},{7,6},{8,9},{9,8},{10,11... | collective-permute-start | bytes 3145736 | tf_op jit(solution)/shard_map/ppermute | solution.py:145
